TPU v7x, 256 devices: a whole 4x4x8 slice. The times are simulated.
256 devices in a mesh: row: 8 (over z), col: 32 (over x, y, core).
Axes of the slice: x: 4, y: 4, z: 8, core: 2. Of those that a mesh axis runs over, the one named last changes fastest.
Arguments:
- tile_values: float32 [8, 32, 128, 128, 128], P('row', 'col')
- tile_coords: int32 [8, 32, 128, 2], P('row', 'col'), may hold values from 0 to 271, as said below
- tile_count: int32 [8, 32], P('row', 'col'), may hold values from 16 to 128, as said below
- objective: float32 [262144], P('col')
- lower: float32 [262144], P('col'), may hold values from -2 to -0.2
- upper: float32 [262144], P('col'), may hold values from 0.2 to 2
- rhs: float32 [278528], P('row')
- primal_start: float32 [262144], P('col'), may hold values from -4 to 4
- dual_start: float32 [278528], P('row'), may hold values from 0 to 1
- step_size: float32 [1], replicated, may hold values from 0.02 to 0.06
Outputs:
- primal_solution: float32 [262144], P('col')
- dual_solution: float32 [278528], P('row')
Inputs may be any that keep to these rules, and one draw needn't show every extreme that they name: `tile_coords`: coordinates are local: block rows 0 to 271, block columns 0 to 63, also in unused slots. Devices whose col index is congruent to their row index modulo the size of row hold one period: their block rows are (col index // size of row) * 64 plus 0 to 63. All other devices hold only linking block rows, 256 to 271. Every block row and every block column of A is met by some used slot. `tile_count`: period devices use all slots; other devices use 16 to 64 slots.
All inputs are finite; a program needn't handle non-finite values.
Results may differ from a plain program's by a relative error of at most 0.00012.
Values sent between devices are 32-bit elements; how exact they have to be, the bound alone decides.
No kernel may reach another device: no remote copies, remote signals or barrier semaphores. Data moves between devices by JAX's collectives and lax.ppermute only.
A program may use at most 64 MiB of HBM per device.

v0:
```python
import jax
import jax.numpy as jnp
from jax import lax
from jax.sharding import PartitionSpec as P

RUIZ = 2
ITERS = 2


EPSILON = 1e-06
HIGHEST = lax.Precision.HIGHEST
HIGH = lax.Precision.HIGH


def butterfly(value, axis, size, combine):
    bit = 1
    while bit < size:
        pairs = [(i, i ^ bit) for i in range(size)]
        value = combine(value, lax.ppermute(value, axis, pairs))
        bit *= 2
    return value


def _max(a, b):
    return jax.tree.map(jnp.maximum, a, b)


def _add(a, b):
    return jax.tree.map(jnp.add, a, b)


def make_local(n_row, n_col):
    def local(
        tile_values,
        tile_coords,
        tile_count,
        objective,
        lower,
        upper,
        rhs,
        primal_start,
        dual_start,
        step_size,
    ):
        tile_width = tile_values.shape[-1]
        slot_count = tile_values.shape[2]
        matrix = tile_values.reshape(slot_count, tile_width, tile_width)
        coords = tile_coords.reshape(slot_count, 2)
        block_rows = coords[:, 0]
        block_cols = coords[:, 1]
        row_blocks = rhs.shape[0] // tile_width
        col_blocks = objective.shape[0] // tile_width
        link_start = col_blocks * (n_col // n_row)
        r = lax.axis_index("row")
        c = lax.axis_index("col")
        is_period = (c % n_row) == r
        seg_start = (c // n_row) * col_blocks
        row_ids = jnp.arange(row_blocks, dtype=jnp.int32)[:, None]
        own_period = is_period & (row_ids >= seg_start) & (row_ids < seg_start + col_blocks)

        in_use = (jnp.arange(slot_count, dtype=jnp.int32) < tile_count.reshape(())).astype(jnp.float32)
        row_onehot = (jnp.arange(row_blocks, dtype=jnp.int32)[:, None] == block_rows[None, :]).astype(
            jnp.float32
        ) * in_use[None, :]
        col_onehot = (jnp.arange(col_blocks, dtype=jnp.int32)[:, None] == block_cols[None, :]).astype(
            jnp.float32
        ) * in_use[None, :]
        magnitude = jnp.abs(matrix) * in_use[:, None, None]

        def row_peaks(col_scale):
            col_pieces = jnp.take(col_scale, block_cols, axis=0)
            row_local = jnp.max(magnitude * col_pieces[:, None, :], axis=2)
            return jnp.zeros((row_blocks, tile_width), jnp.float32).at[block_rows].max(row_local)

        def col_peaks(row_scale):
            row_pieces = jnp.take(row_scale, block_rows, axis=0)
            col_local = jnp.max(magnitude * row_pieces[:, :, None], axis=1)
            return jnp.zeros((col_blocks, tile_width), jnp.float32).at[block_cols].max(col_local)

        def rescale(scale, peak):
            return scale / jnp.sqrt(scale * peak + EPSILON)

        rhs_b = rhs.reshape(row_blocks, tile_width)
        obj_b = objective.reshape(col_blocks, tile_width)
        lanes = jnp.arange(tile_width, dtype=jnp.int32)[None, :]

        row_scale0 = jnp.ones((row_blocks, tile_width), jnp.float32)
        col_scale0 = jnp.ones((col_blocks, tile_width), jnp.float32)
        row_local1 = row_peaks(col_scale0)
        link_peak1 = butterfly(row_local1[link_start:], "col", n_col, _max)
        row_scale1 = rescale(row_scale0, jnp.concatenate([row_local1[:link_start], link_peak1], axis=0))
        col_local1 = col_peaks(row_scale0)
        col_local2 = col_peaks(row_scale1)
        col_both = butterfly(jnp.concatenate([col_local1, col_local2], axis=0), "row", n_row, _max)
        col_scale1 = rescale(col_scale0, col_both[:col_blocks])
        col_scale = rescale(col_scale1, col_both[col_blocks:])

        row_local2 = row_peaks(col_scale1)
        own_scale2 = rescale(row_scale1, row_local2)
        own_bound = own_scale2 * rhs_b
        period_square = jnp.sum(jnp.where(own_period, own_bound * own_bound, 0.0))
        cost = col_scale * obj_b
        cost_square = jnp.sum(cost * cost)
        slot = jnp.where(lanes == c, cost_square, 0.0)
        slot = jnp.where(is_period & (lanes == n_col + c // n_row), period_square, slot)
        packed2 = butterfly(jnp.concatenate([row_local2[link_start:], slot], axis=0), "col", n_col, _max)
        link_peak2 = packed2[: row_blocks - link_start]
        spare = packed2[row_blocks - link_start]
        cost_total = jnp.sum(spare[:n_col]).reshape(1)
        period_total = jnp.sum(spare[n_col : n_col + n_col // n_row]).reshape(1)
        row_scale = rescale(row_scale1, jnp.concatenate([row_local2[:link_start], link_peak2], axis=0))

        bound = row_scale * rhs_b
        low_scaled = lower.reshape(col_blocks, tile_width) / col_scale
        high_scaled = upper.reshape(col_blocks, tile_width) / col_scale
        primal = primal_start.reshape(col_blocks, tile_width) / col_scale
        dual = dual_start.reshape(row_blocks, tile_width) / row_scale
        link_bound = bound[link_start:]
        bound_part = period_total + jnp.sum(link_bound * link_bound).reshape(1)

        def adjoint_local(dual):
            pieces = jnp.take(row_scale * dual, block_rows, axis=0)
            products = jnp.einsum("tij,ti->tj", matrix, pieces, precision=HIGH)
            return jnp.dot(col_onehot, products, precision=HIGHEST)

        def forward_local(extra):
            forward_pieces = jnp.take(col_scale * extra, block_cols, axis=0)
            forward_products = jnp.einsum("tij,tj->ti", matrix, forward_pieces, precision=HIGH)
            return jnp.dot(row_onehot, forward_products, precision=HIGHEST)

        image0_part = adjoint_local(dual)
        bound_row = jnp.where(lanes == 0, bound_part[0], 0.0)
        packed3 = butterfly(jnp.concatenate([image0_part, bound_row], axis=0), "row", n_row, _add)
        image = packed3[:col_blocks]
        bound_total = packed3[col_blocks, :1]
        weight = jnp.sqrt(cost_total[0] + EPSILON) / jnp.sqrt(bound_total[0] + EPSILON)
        primal_step = step_size[0] / weight
        dual_step = step_size[0] * weight

        for iteration in range(ITERS):
            if iteration > 0:
                image = butterfly(adjoint_local(dual), "row", n_row, _add)
            moved = jnp.clip(primal - primal_step * (cost - col_scale * image), low_scaled, high_scaled)
            extra = 2.0 * moved - primal
            partial_rows = forward_local(extra)
            primal = moved
            if iteration < ITERS - 1:
                link_total = butterfly(partial_rows[link_start:], "col", n_col, _add)
                total = jnp.concatenate([partial_rows[:link_start], link_total], axis=0)
                dual = jnp.maximum(dual + dual_step * (bound - row_scale * total), 0.0)
            else:
                own_dual = jnp.maximum(dual + dual_step * (bound - row_scale * partial_rows), 0.0)
                own_out = jnp.where(own_period, row_scale * own_dual, 0.0)
                joined = butterfly(
                    jnp.concatenate([own_out[:link_start], partial_rows[link_start:]], axis=0),
                    "col",
                    n_col,
                    _add,
                )
                link_dual = jnp.maximum(
                    dual[link_start:]
                    + dual_step * (bound[link_start:] - row_scale[link_start:] * joined[link_start:]),
                    0.0,
                )
                dual_out = jnp.concatenate([joined[:link_start], row_scale[link_start:] * link_dual], axis=0)
        return ((col_scale * primal).reshape(-1), dual_out.reshape(-1))

    return local


def solution(mesh):
    placed = (
        P("row", "col", None, None, None),
        P("row", "col", None, None),
        P("row", "col"),
        P("col"),
        P("col"),
        P("col"),
        P("row"),
        P("col"),
        P("row"),
        P(),
    )
    local = make_local(mesh.shape["row"], mesh.shape["col"])
    return jax.shard_map(
        local, mesh=mesh, in_specs=placed, out_specs=(P("col"), P("row")), check_vma=False
    )
```

profile of v0, /device:TPU:8, one launch (start us, length us, event | category | flops | bytes accessed | tf_op | source)
XLA Modules:
  0.0 209.2 jit_solution(16740800065155614779)
XLA Ops:
  3.6 5.8 %multiply_reduce_fusion.2 = f32[128,128]{1,0:T(8,128)S(1)} fusion(f32[1,1,128,128,128]{4,3,2,1,0:T(8,128)} %param.14, f32[128,128]{1,0:T(8,128)S(1)} %broadcast_select_fusion.6, f32[128]{0:T(128)S(1)} %compare_convert_fusion), kind=kLoop, calls=%fused_computation.24 | loop fusion | flops 8372224 | bytes 8520192 | tf_op jit(solution)/shard_map/reduce_max | solution.py:72
  17.6 3.0 %collective-permute-done.2 = f32[16,128]{1,0:T(8,128)S(1)} collective-permute-done((f32[16,128]{1,0:T(8,128)S(1)}, f32[16,128]{1,0:T(8,128)S(1)}, u32[]{:S(2)}, u32[]{:S(2)}) %collective-permute-start.2) | collective-permute-done | bytes 8224 | tf_op jit(solution)/shard_map/ppermute | solution.py:19
  24.3 3.0 %collective-permute-start.4 = (f32[16,128]{1,0:T(8,128)S(1)}, f32[16,128]{1,0:T(8,128)S(1)}, u32[]{:S(2)}, u32[]{:S(2)}) collective-permute-start(f32[16,128]{1,0:T(8,128)S(1)} %max.69), channel_id=1, source_target_pairs={{0,16},{1,17},{2,18},{3,19},{4,20},{5,21},{6,22},{7,23},{8,24},{9,... | collective-permute-start | bytes 24584 | tf_op jit(solution)/shard_map/ppermute | solution.py:19
  30.2 8.8 %multiply_reduce_fusion.1 = (f32[128,128]{1,0:T(8,128)S(1)}, f32[128,128]{1,0:T(8,128)S(1)}) fusion(f32[1,1,128,128,128]{4,3,2,1,0:T(8,128)} %param.14, f32[128,128]{1,0:T(8,128)S(1)} %get-tuple-element.26, f32[128]{0:T(128)S(1)} %compare_convert_fusion, f32[128,128]{1,0:T(8,128)S(1)} %get-tuple-element.25), kind=kLoop, calls=%fused_computation.23 | loop fusion | flops 12550144 | bytes 8651264 | tf_op jit(solution)/shard_map/reduce_max | solution.py:77
  42.9 2.6 %collective-permute-done.5 = f32[128,128]{1,0:T(8,128)S(1)} collective-permute-done((f32[128,128]{1,0:T(8,128)S(1)}, f32[128,128]{1,0:T(8,128)S(1)}, u32[]{:S(2)}, u32[]{:S(2)}) %collective-permute-start.5) | collective-permute-done | bytes 65568 | tf_op jit(solution)/shard_map/ppermute | solution.py:19
  45.5 3.1 %collective-permute-start.6 = (f32[128,128]{1,0:T(8,128)S(1)}, f32[128,128]{1,0:T(8,128)S(1)}, u32[]{:S(2)}, u32[]{:S(2)}) collective-permute-start(f32[128,128]{1,0:T(8,128)S(1)} %max.71), channel_id=1, source_target_pairs={{0,64},{32,96},{64,0},{96,32},{128,192},{160,224},{192,128},{224,1... | collective-permute-start | bytes 196616 | tf_op jit(solution)/shard_map/ppermute | solution.py:19
  50.9 8.6 %collective-permute-start.7 = (f32[128,128]{1,0:T(8,128)S(1)}, f32[128,128]{1,0:T(8,128)S(1)}, u32[]{:S(2)}, u32[]{:S(2)}) collective-permute-start(f32[128,128]{1,0:T(8,128)S(1)} %max.72), channel_id=1, source_target_pairs={{0,128},{32,160},{64,192},{96,224},{128,0},{160,32},{192,64},{224,... | collective-permute-start | bytes 196616 | tf_op jit(solution)/shard_map/ppermute | solution.py:19
  63.2 5.8 %multiply_reduce_fusion = f32[128,128]{1,0:T(8,128)S(1)} fusion(f32[1,1,128,128,128]{4,3,2,1,0:T(8,128)} %param.14, f32[128,128]{1,0:T(8,128)S(1)} %broadcast_select_fusion.4, f32[128]{0:T(128)S(1)} %compare_convert_fusion), kind=kLoop, calls=%fused_computation.22 | loop fusion | flops 8372224 | bytes 8520192 | tf_op jit(solution)/shard_map/reduce_max | solution.py:72
  74.2 2.8 %collective-permute-done.9 = f32[17,128]{1,0:T(8,128)S(1)} collective-permute-done((f32[17,128]{1,0:T(8,128)S(1)}, f32[17,128]{1,0:T(8,128)S(1)}, u32[]{:S(2)}, u32[]{:S(2)}) %collective-permute-start.9) | collective-permute-done | bytes 8736 | tf_op jit(solution)/shard_map/ppermute | solution.py:19
  77.0 2.3 %collective-permute-start.10 = (f32[17,128]{1,0:T(8,128)S(1)}, f32[17,128]{1,0:T(8,128)S(1)}, u32[]{:S(2)}, u32[]{:S(2)}) collective-permute-start(f32[17,128]{1,0:T(8,128)S(1)} %max.75), channel_id=1, source_target_pairs={{0,4},{1,5},{2,6},{3,7},{4,0},{5,1},{6,2},{7,3},{8,12},{9,13},{10,... | collective-permute-start | bytes 26120 | tf_op jit(solution)/shard_map/ppermute | solution.py:19
  79.3 2.9 %collective-permute-done.10 = f32[17,128]{1,0:T(8,128)S(1)} collective-permute-done((f32[17,128]{1,0:T(8,128)S(1)}, f32[17,128]{1,0:T(8,128)S(1)}, u32[]{:S(2)}, u32[]{:S(2)}) %collective-permute-start.10) | collective-permute-done | bytes 8736 | tf_op jit(solution)/shard_map/ppermute | solution.py:19
  85.9 3.1 %collective-permute-start.12 = (f32[17,128]{1,0:T(8,128)S(1)}, f32[17,128]{1,0:T(8,128)S(1)}, u32[]{:S(2)}, u32[]{:S(2)}) collective-permute-start(f32[17,128]{1,0:T(8,128)S(1)} %max.77), channel_id=1, source_target_pairs={{0,16},{1,17},{2,18},{3,19},{4,20},{5,21},{6,22},{7,23},{8,24},{9,... | collective-permute-start | bytes 26120 | tf_op jit(solution)/shard_map/ppermute | solution.py:19
  92.6 5.7 %fusion.6 = f32[128,1,128]{2,1,0:T(1,128)S(1)} fusion(f32[128,128,1]{1,2,0:T(1,128)S(1)} %bitcast.136, f32[1,1,128,128,128]{4,3,2,1,0:T(8,128)} %param.14), kind=kOutput, calls=%fused_computation.18 | convolution fusion | flops 12582912 | bytes 8519680 | tf_op jit(solution)/shard_map/tij,ti->tj/dot_general | solution.py:123
  100.6 3.9 %collective-permute-done.13 = f32[65,128]{1,0:T(8,128)S(1)} collective-permute-done((f32[65,128]{1,0:T(8,128)S(1)}, f32[65,128]{1,0:T(8,128)S(1)}, u32[]{:S(2)}, u32[]{:S(2)}) %collective-permute-start.13) | collective-permute-done | bytes 33312 | tf_op jit(solution)/shard_map/ppermute | solution.py:19
  106.5 3.5 %collective-permute-done.14 = f32[65,128]{1,0:T(8,128)S(1)} collective-permute-done((f32[65,128]{1,0:T(8,128)S(1)}, f32[65,128]{1,0:T(8,128)S(1)}, u32[]{:S(2)}, u32[]{:S(2)}) %collective-permute-start.14) | collective-permute-done | bytes 33312 | tf_op jit(solution)/shard_map/ppermute | solution.py:19
  110.0 5.8 %collective-permute-start.15 = (f32[65,128]{1,0:T(8,128)S(1)}, f32[65,128]{1,0:T(8,128)S(1)}, u32[]{:S(2)}, u32[]{:S(2)}) collective-permute-start(f32[65,128]{1,0:T(8,128)S(1)} %add.125), channel_id=1, source_target_pairs={{0,128},{32,160},{64,192},{96,224},{128,0},{160,32},{192,64},{224,... | collective-permute-start | bytes 99848 | tf_op jit(solution)/shard_map/ppermute | solution.py:19
  119.9 8.9 %fusion.4 = f32[128,1,128]{2,1,0:T(1,128)S(1)} fusion(f32[128,128,1]{1,2,0:T(1,128)S(1)} %bitcast.137, f32[1,1,128,128,128]{4,3,2,1,0:T(8,128)} %param.14), kind=kOutput, calls=%fused_computation.16 | convolution fusion | flops 12582912 | bytes 8519680 | tf_op jit(solution)/shard_map/tij,tj->ti/dot_general | solution.py:128
  131.0 3.0 %collective-permute-done.17 = f32[16,128]{1,0:T(8,128)S(1)} collective-permute-done((f32[16,128]{1,0:T(8,128)S(1)}, f32[16,128]{1,0:T(8,128)S(1)}, u32[]{:S(2)}, u32[]{:S(2)}) %collective-permute-start.17) | collective-permute-done | bytes 8224 | tf_op jit(solution)/shard_map/ppermute | solution.py:19
  134.0 2.3 %collective-permute-start.18 = (f32[16,128]{1,0:T(8,128)S(1)}, f32[16,128]{1,0:T(8,128)S(1)}, u32[]{:S(2)}, u32[]{:S(2)}) collective-permute-start(f32[16,128]{1,0:T(8,128)S(1)} %add.129), channel_id=1, source_target_pairs={{0,4},{1,5},{2,6},{3,7},{4,0},{5,1},{6,2},{7,3},{8,12},{9,13},{10,... | collective-permute-start | bytes 24584 | tf_op jit(solution)/shard_map/ppermute | solution.py:19
  136.3 2.9 %collective-permute-done.18 = f32[16,128]{1,0:T(8,128)S(1)} collective-permute-done((f32[16,128]{1,0:T(8,128)S(1)}, f32[16,128]{1,0:T(8,128)S(1)}, u32[]{:S(2)}, u32[]{:S(2)}) %collective-permute-start.18) | collective-permute-done | bytes 8224 | tf_op jit(solution)/shard_map/ppermute | solution.py:19
  142.8 3.3 %collective-permute-start.20 = (f32[16,128]{1,0:T(8,128)S(1)}, f32[16,128]{1,0:T(8,128)S(1)}, u32[]{:S(2)}, u32[]{:S(2)}) collective-permute-start(f32[16,128]{1,0:T(8,128)S(1)} %add.131), channel_id=1, source_target_pairs={{0,16},{1,17},{2,18},{3,19},{4,20},{5,21},{6,22},{7,23},{8,24},{9,... | collective-permute-start | bytes 24584 | tf_op jit(solution)/shard_map/ppermute | solution.py:19
  148.8 5.7 %fusion.2 = f32[128,1,128]{2,1,0:T(1,128)S(1)} fusion(f32[128,128,1]{1,2,0:T(1,128)S(1)} %bitcast.133, f32[1,1,128,128,128]{4,3,2,1,0:T(8,128)} %param.14), kind=kOutput, calls=%fused_computation.14 | convolution fusion | flops 12582912 | bytes 8519680 | tf_op jit(solution)/shard_map/tij,ti->tj/dot_general | solution.py:123
  154.7 3.9 %collective-permute-done.21 = f32[64,128]{1,0:T(8,128)S(1)} collective-permute-done((f32[64,128]{1,0:T(8,128)S(1)}, f32[64,128]{1,0:T(8,128)S(1)}, u32[]{:S(2)}, u32[]{:S(2)}) %collective-permute-start.21) | collective-permute-done | bytes 32800 | tf_op jit(solution)/shard_map/ppermute | solution.py:19
  159.7 4.2 %collective-permute-done.22 = f32[64,128]{1,0:T(8,128)S(1)} collective-permute-done((f32[64,128]{1,0:T(8,128)S(1)}, f32[64,128]{1,0:T(8,128)S(1)}, u32[]{:S(2)}, u32[]{:S(2)}) %collective-permute-start.22) | collective-permute-done | bytes 32800 | tf_op jit(solution)/shard_map/ppermute | solution.py:19
  163.9 5.6 %collective-permute-start.23 = (f32[64,128]{1,0:T(8,128)S(1)}, f32[64,128]{1,0:T(8,128)S(1)}, u32[]{:S(2)}, u32[]{:S(2)}) collective-permute-start(f32[64,128]{1,0:T(8,128)S(1)} %add.135), channel_id=1, source_target_pairs={{0,128},{32,160},{64,192},{96,224},{128,0},{160,32},{192,64},{224,... | collective-permute-start | bytes 98312 | tf_op jit(solution)/shard_map/ppermute | solution.py:19
  173.1 8.9 %fusion = f32[128,1,128]{2,1,0:T(1,128)S(1)} fusion(f32[128,128,1]{1,2,0:T(1,128)S(1)} %bitcast.135, f32[1,1,128,128,128]{4,3,2,1,0:T(8,128)} %param.14), kind=kOutput, calls=%fused_computation.12 | convolution fusion | flops 12582912 | bytes 8519680 | tf_op jit(solution)/shard_map/tij,tj->ti/dot_general | solution.py:128
  184.8 5.2 %collective-permute-done.25 = f32[272,128]{1,0:T(8,128)S(1)} collective-permute-done((f32[272,128]{1,0:T(8,128)S(1)}, f32[272,128]{1,0:T(8,128)S(1)}, u32[]{:S(2)}, u32[]{:S(2)}) %collective-permute-start.25) | collective-permute-done | bytes 139296 | tf_op jit(solution)/shard_map/ppermute | solution.py:19
  190.0 2.4 %collective-permute-start.26 = (f32[272,128]{1,0:T(8,128)S(1)}, f32[272,128]{1,0:T(8,128)S(1)}, u32[]{:S(2)}, u32[]{:S(2)}) collective-permute-start(f32[272,128]{1,0:T(8,128)S(1)} %add.139), channel_id=1, source_target_pairs={{0,4},{1,5},{2,6},{3,7},{4,0},{5,1},{6,2},{7,3},{8,12},{9,13},{10,... | collective-permute-start | bytes 417800 | tf_op jit(solution)/shard_map/ppermute | solution.py:19
  192.4 4.3 %collective-permute-done.26 = f32[272,128]{1,0:T(8,128)S(1)} collective-permute-done((f32[272,128]{1,0:T(8,128)S(1)}, f32[272,128]{1,0:T(8,128)S(1)}, u32[]{:S(2)}, u32[]{:S(2)}) %collective-permute-start.26) | collective-permute-done | bytes 139296 | tf_op jit(solution)/shard_map/ppermute | solution.py:19
  198.3 3.5 %collective-permute-done.27 = f32[272,128]{1,0:T(8,128)S(1)} collective-permute-done((f32[272,128]{1,0:T(8,128)S(1)}, f32[272,128]{1,0:T(8,128)S(1)}, u32[]{:S(2)}, u32[]{:S(2)}) %collective-permute-start.27) | collective-permute-done | bytes 139296 | tf_op jit(solution)/shard_map/ppermute | solution.py:19
  201.9 3.3 %collective-permute-start.28 = (f32[272,128]{1,0:T(8,128)S(1)}, f32[272,128]{1,0:T(8,128)S(1)}, u32[]{:S(2)}, u32[]{:S(2)}) collective-permute-start(f32[272,128]{1,0:T(8,128)S(1)} %add.141), channel_id=1, source_target_pairs={{0,16},{1,17},{2,18},{3,19},{4,20},{5,21},{6,22},{7,23},{8,24},{9,... | collective-permute-start | bytes 417800 | tf_op jit(solution)/shard_map/ppermute | solution.py:19
  205.1 3.4 %collective-permute-done.28 = f32[272,128]{1,0:T(8,128)S(1)} collective-permute-done((f32[272,128]{1,0:T(8,128)S(1)}, f32[272,128]{1,0:T(8,128)S(1)}, u32[]{:S(2)}, u32[]{:S(2)}) %collective-permute-start.28) | collective-permute-done | bytes 139296 | tf_op jit(solution)/shard_map/ppermute | solution.py:19
  (135 shorter events, 62.9 us)
Async XLA Ops:
  3.6 58.2 %copy-start.2 = (f32[8192]{0:T(1024)S(1)}, f32[8192]{0:T(1024)}, u32[]{:S(2)}) copy-start(f32[8192]{0:T(1024)} %param.17) | copy-start | bytes 98308
  10.4 1.3 collective-permute-start
  11.7 3.8 %collective-permute-start.1 = (f32[16,128]{1,0:T(8,128)S(1)}, f32[16,128]{1,0:T(8,128)S(1)}, u32[]{:S(2)}, u32[]{:S(2)}) collective-permute-start(f32[16,128]{1,0:T(8,128)S(1)} %slice_maximum_fusion), channel_id=1, source_target_pairs={{0,2},{1,3},{2,0},{3,1},{4,6},{5,7},{6,4},{7,5},{8,10},{9,11},{10,... | collective-permute-start | bytes 24584 | tf_op jit(solution)/shard_map/ppermute | solution.py:19
  15.5 5.2 %collective-permute-start.2 = (f32[16,128]{1,0:T(8,128)S(1)}, f32[16,128]{1,0:T(8,128)S(1)}, u32[]{:S(2)}, u32[]{:S(2)}) collective-permute-start(f32[16,128]{1,0:T(8,128)S(1)} %max.67), channel_id=1, source_target_pairs={{0,4},{1,5},{2,6},{3,7},{4,0},{5,1},{6,2},{7,3},{8,12},{9,13},{10,... | collective-permute-start | bytes 24584 | tf_op jit(solution)/shard_map/ppermute | solution.py:19
  20.6 3.7 %collective-permute-start.3 = (f32[16,128]{1,0:T(8,128)S(1)}, f32[16,128]{1,0:T(8,128)S(1)}, u32[]{:S(2)}, u32[]{:S(2)}) collective-permute-start(f32[16,128]{1,0:T(8,128)S(1)} %max.68), channel_id=1, source_target_pairs={{0,8},{1,9},{2,10},{3,11},{4,12},{5,13},{6,14},{7,15},{8,0},{9,1},... | collective-permute-start | bytes 24584 | tf_op jit(solution)/shard_map/ppermute | solution.py:19
  24.3 5.2 %collective-permute-start.4 = (f32[16,128]{1,0:T(8,128)S(1)}, f32[16,128]{1,0:T(8,128)S(1)}, u32[]{:S(2)}, u32[]{:S(2)}) collective-permute-start(f32[16,128]{1,0:T(8,128)S(1)} %max.69), channel_id=1, source_target_pairs={{0,16},{1,17},{2,18},{3,19},{4,20},{5,21},{6,22},{7,23},{8,24},{9,... | collective-permute-start | bytes 24584 | tf_op jit(solution)/shard_map/ppermute | solution.py:19
  30.2 61.6 %copy-start.1 = (f32[34816]{0:T(1024)S(1)}, f32[34816]{0:T(1024)}, u32[]{:S(2)}) copy-start(f32[34816]{0:T(1024)} %param.22) | copy-start | bytes 417796
  41.1 4.4 %collective-permute-start.5 = (f32[128,128]{1,0:T(8,128)S(1)}, f32[128,128]{1,0:T(8,128)S(1)}, u32[]{:S(2)}, u32[]{:S(2)}) collective-permute-start(f32[128,128]{1,0:T(8,128)S(1)} %constant_dynamic-update-slice_fusion), channel_id=1, source_target_pairs={{0,32},{32,0},{64,96},{96,64},{128,160},{160,128},{192,224},{224,1... | collective-permute-start | bytes 196616 | tf_op jit(solution)/shard_map/ppermute | solution.py:19
  45.5 5.4 %collective-permute-start.6 = (f32[128,128]{1,0:T(8,128)S(1)}, f32[128,128]{1,0:T(8,128)S(1)}, u32[]{:S(2)}, u32[]{:S(2)}) collective-permute-start(f32[128,128]{1,0:T(8,128)S(1)} %max.71), channel_id=1, source_target_pairs={{0,64},{32,96},{64,0},{96,32},{128,192},{160,224},{192,128},{224,1... | collective-permute-start | bytes 196616 | tf_op jit(solution)/shard_map/ppermute | solution.py:19
  50.9 10.9 %collective-permute-start.7 = (f32[128,128]{1,0:T(8,128)S(1)}, f32[128,128]{1,0:T(8,128)S(1)}, u32[]{:S(2)}, u32[]{:S(2)}) collective-permute-start(f32[128,128]{1,0:T(8,128)S(1)} %max.72), channel_id=1, source_target_pairs={{0,128},{32,160},{64,192},{96,224},{128,0},{160,32},{192,64},{224,... | collective-permute-start | bytes 196616 | tf_op jit(solution)/shard_map/ppermute | solution.py:19
  63.2 55.9 %copy-start.3 = (f32[8192]{0:T(1024)S(1)}, f32[8192]{0:T(1024)}, u32[]{:S(2)}) copy-start(f32[8192]{0:T(1024)} %param.19) | copy-start | bytes 98308
  72.1 1.3 collective-permute-start.8
  73.3 3.7 %collective-permute-start.9 = (f32[17,128]{1,0:T(8,128)S(1)}, f32[17,128]{1,0:T(8,128)S(1)}, u32[]{:S(2)}, u32[]{:S(2)}) collective-permute-start(f32[17,128]{1,0:T(8,128)S(1)} %fusion.74), channel_id=1, source_target_pairs={{0,2},{1,3},{2,0},{3,1},{4,6},{5,7},{6,4},{7,5},{8,10},{9,11},{10,... | collective-permute-start | bytes 26120 | tf_op jit(solution)/shard_map/ppermute | solution.py:19
  77.0 5.2 %collective-permute-start.10 = (f32[17,128]{1,0:T(8,128)S(1)}, f32[17,128]{1,0:T(8,128)S(1)}, u32[]{:S(2)}, u32[]{:S(2)}) collective-permute-start(f32[17,128]{1,0:T(8,128)S(1)} %max.75), channel_id=1, source_target_pairs={{0,4},{1,5},{2,6},{3,7},{4,0},{5,1},{6,2},{7,3},{8,12},{9,13},{10,... | collective-permute-start | bytes 26120 | tf_op jit(solution)/shard_map/ppermute | solution.py:19
  82.2 3.7 %collective-permute-start.11 = (f32[17,128]{1,0:T(8,128)S(1)}, f32[17,128]{1,0:T(8,128)S(1)}, u32[]{:S(2)}, u32[]{:S(2)}) collective-permute-start(f32[17,128]{1,0:T(8,128)S(1)} %max.76), channel_id=1, source_target_pairs={{0,8},{1,9},{2,10},{3,11},{4,12},{5,13},{6,14},{7,15},{8,0},{9,1},... | collective-permute-start | bytes 26120 | tf_op jit(solution)/shard_map/ppermute | solution.py:19
  85.9 5.2 %collective-permute-start.12 = (f32[17,128]{1,0:T(8,128)S(1)}, f32[17,128]{1,0:T(8,128)S(1)}, u32[]{:S(2)}, u32[]{:S(2)}) collective-permute-start(f32[17,128]{1,0:T(8,128)S(1)} %max.77), channel_id=1, source_target_pairs={{0,16},{1,17},{2,18},{3,19},{4,20},{5,21},{6,22},{7,23},{8,24},{9,... | collective-permute-start | bytes 26120 | tf_op jit(solution)/shard_map/ppermute | solution.py:19
  100.5 4.0 %collective-permute-start.13 = (f32[65,128]{1,0:T(8,128)S(1)}, f32[65,128]{1,0:T(8,128)S(1)}, u32[]{:S(2)}, u32[]{:S(2)}) collective-permute-start(f32[65,128]{1,0:T(8,128)S(1)} %pad_maximum_fusion.1), channel_id=1, source_target_pairs={{0,32},{32,0},{64,96},{96,64},{128,160},{160,128},{192,224},{224,1... | collective-permute-start | bytes 99848 | tf_op jit(solution)/shard_map/ppermute | solution.py:19
  104.5 5.4 %collective-permute-start.14 = (f32[65,128]{1,0:T(8,128)S(1)}, f32[65,128]{1,0:T(8,128)S(1)}, u32[]{:S(2)}, u32[]{:S(2)}) collective-permute-start(f32[65,128]{1,0:T(8,128)S(1)} %fusion.75), channel_id=1, source_target_pairs={{0,64},{32,96},{64,0},{96,32},{128,192},{160,224},{192,128},{224,1... | collective-permute-start | bytes 99848 | tf_op jit(solution)/shard_map/ppermute | solution.py:19
  110.0 7.9 %collective-permute-start.15 = (f32[65,128]{1,0:T(8,128)S(1)}, f32[65,128]{1,0:T(8,128)S(1)}, u32[]{:S(2)}, u32[]{:S(2)}) collective-permute-start(f32[65,128]{1,0:T(8,128)S(1)} %add.125), channel_id=1, source_target_pairs={{0,128},{32,160},{64,192},{96,224},{128,0},{160,32},{192,64},{224,... | collective-permute-start | bytes 99848 | tf_op jit(solution)/shard_map/ppermute | solution.py:19
  129.1 1.3 collective-permute-start.16
  130.3 3.7 %collective-permute-start.17 = (f32[16,128]{1,0:T(8,128)S(1)}, f32[16,128]{1,0:T(8,128)S(1)}, u32[]{:S(2)}, u32[]{:S(2)}) collective-permute-start(f32[16,128]{1,0:T(8,128)S(1)} %slice_add_fusion.2), channel_id=1, source_target_pairs={{0,2},{1,3},{2,0},{3,1},{4,6},{5,7},{6,4},{7,5},{8,10},{9,11},{10,... | collective-permute-start | bytes 24584 | tf_op jit(solution)/shard_map/ppermute | solution.py:19
  134.0 5.2 %collective-permute-start.18 = (f32[16,128]{1,0:T(8,128)S(1)}, f32[16,128]{1,0:T(8,128)S(1)}, u32[]{:S(2)}, u32[]{:S(2)}) collective-permute-start(f32[16,128]{1,0:T(8,128)S(1)} %add.129), channel_id=1, source_target_pairs={{0,4},{1,5},{2,6},{3,7},{4,0},{5,1},{6,2},{7,3},{8,12},{9,13},{10,... | collective-permute-start | bytes 24584 | tf_op jit(solution)/shard_map/ppermute | solution.py:19
  139.2 3.7 %collective-permute-start.19 = (f32[16,128]{1,0:T(8,128)S(1)}, f32[16,128]{1,0:T(8,128)S(1)}, u32[]{:S(2)}, u32[]{:S(2)}) collective-permute-start(f32[16,128]{1,0:T(8,128)S(1)} %add.130), channel_id=1, source_target_pairs={{0,8},{1,9},{2,10},{3,11},{4,12},{5,13},{6,14},{7,15},{8,0},{9,1},... | collective-permute-start | bytes 24584 | tf_op jit(solution)/shard_map/ppermute | solution.py:19
  142.8 5.2 %collective-permute-start.20 = (f32[16,128]{1,0:T(8,128)S(1)}, f32[16,128]{1,0:T(8,128)S(1)}, u32[]{:S(2)}, u32[]{:S(2)}) collective-permute-start(f32[16,128]{1,0:T(8,128)S(1)} %add.131), channel_id=1, source_target_pairs={{0,16},{1,17},{2,18},{3,19},{4,20},{5,21},{6,22},{7,23},{8,24},{9,... | collective-permute-start | bytes 24584 | tf_op jit(solution)/shard_map/ppermute | solution.py:19
  154.6 4.0 %collective-permute-start.21 = (f32[64,128]{1,0:T(8,128)S(1)}, f32[64,128]{1,0:T(8,128)S(1)}, u32[]{:S(2)}, u32[]{:S(2)}) collective-permute-start(f32[64,128]{1,0:T(8,128)S(1)} %fusion.38), channel_id=1, source_target_pairs={{0,32},{32,0},{64,96},{96,64},{128,160},{160,128},{192,224},{224,1... | collective-permute-start | bytes 98312 | tf_op jit(solution)/shard_map/ppermute | solution.py:19
  158.6 5.3 %collective-permute-start.22 = (f32[64,128]{1,0:T(8,128)S(1)}, f32[64,128]{1,0:T(8,128)S(1)}, u32[]{:S(2)}, u32[]{:S(2)}) collective-permute-start(f32[64,128]{1,0:T(8,128)S(1)} %add.134), channel_id=1, source_target_pairs={{0,64},{32,96},{64,0},{96,32},{128,192},{160,224},{192,128},{224,1... | collective-permute-start | bytes 98312 | tf_op jit(solution)/shard_map/ppermute | solution.py:19
  163.9 7.8 %collective-permute-start.23 = (f32[64,128]{1,0:T(8,128)S(1)}, f32[64,128]{1,0:T(8,128)S(1)}, u32[]{:S(2)}, u32[]{:S(2)}) collective-permute-start(f32[64,128]{1,0:T(8,128)S(1)} %add.135), channel_id=1, source_target_pairs={{0,128},{32,160},{64,192},{96,224},{128,0},{160,32},{192,64},{224,... | collective-permute-start | bytes 98312 | tf_op jit(solution)/shard_map/ppermute | solution.py:19
  182.5 1.7 collective-permute-start.24
  184.2 5.8 %collective-permute-start.25 = (f32[272,128]{1,0:T(8,128)S(1)}, f32[272,128]{1,0:T(8,128)S(1)}, u32[]{:S(2)}, u32[]{:S(2)}) collective-permute-start(f32[272,128]{1,0:T(8,128)S(1)} %fusion.76), channel_id=1, source_target_pairs={{0,2},{1,3},{2,0},{3,1},{4,6},{5,7},{6,4},{7,5},{8,10},{9,11},{10,... | collective-permute-start | bytes 417800 | tf_op jit(solution)/shard_map/ppermute | solution.py:19
  190.0 6.6 %collective-permute-start.26 = (f32[272,128]{1,0:T(8,128)S(1)}, f32[272,128]{1,0:T(8,128)S(1)}, u32[]{:S(2)}, u32[]{:S(2)}) collective-permute-start(f32[272,128]{1,0:T(8,128)S(1)} %add.139), channel_id=1, source_target_pairs={{0,4},{1,5},{2,6},{3,7},{4,0},{5,1},{6,2},{7,3},{8,12},{9,13},{10,... | collective-permute-start | bytes 417800 | tf_op jit(solution)/shard_map/ppermute | solution.py:19
  196.7 5.1 %collective-permute-start.27 = (f32[272,128]{1,0:T(8,128)S(1)}, f32[272,128]{1,0:T(8,128)S(1)}, u32[]{:S(2)}, u32[]{:S(2)}) collective-permute-start(f32[272,128]{1,0:T(8,128)S(1)} %add.140), channel_id=1, source_target_pairs={{0,8},{1,9},{2,10},{3,11},{4,12},{5,13},{6,14},{7,15},{8,0},{9,1},... | collective-permute-start | bytes 417800 | tf_op jit(solution)/shard_map/ppermute | solution.py:19
  201.9 6.6 %collective-permute-start.28 = (f32[272,128]{1,0:T(8,128)S(1)}, f32[272,128]{1,0:T(8,128)S(1)}, u32[]{:S(2)}, u32[]{:S(2)}) collective-permute-start(f32[272,128]{1,0:T(8,128)S(1)} %add.141), channel_id=1, source_target_pairs={{0,16},{1,17},{2,18},{3,19},{4,20},{5,21},{6,22},{7,23},{8,24},{9,... | collective-permute-start | bytes 417800 | tf_op jit(solution)/shard_map/ppermute | solution.py:19
  (3 other events, 151.6 us)
where the time goes:
time: 211 us; the launch traced here: 209 us
  waiting for transfers between devices  75.1 us (36%)
  starting transfers between devices  60.2 us (29%)
  other arithmetic  32.9 us (16%)
  matrix products  30.1 us (14%)
  local copies, waits for them, and re-layouts  5.8 us (3%)
  between operations  5.17 us (2%)
    ppermute x29, waiting for transfers between devices, butterfly(): value = combine(value, lax.ppermute(value, axis, pairs))  75.1 us
    ppermute x29, starting transfers between devices, butterfly(): value = combine(value, lax.ppermute(value, axis, pairs))  60.2 us
    dot_general x2, matrix products, forward_local(): jnp.einsum('tij,tj->ti', matrix, forward_pieces, precision=HIGH)  17.8 us
    reduce_max x2, other arithmetic, row_peaks(): row_local = jnp.max(magnitude * col_pieces[:, None, :], axis=2)  11.6 us
    dot_general x2, matrix products, adjoint_local(): products = jnp.einsum('tij,ti->tj', matrix, pieces, precision=HIGH)  11.3 us
    reduce_max x1, other arithmetic, col_peaks(): col_local = jnp.max(magnitude * row_pieces[:, :, None], axis=1)  8.75 us
  transfers between devices with their start and end apart: 29, of which 29 were waited for; matrix products, arithmetic and copies ran while one was open for 1% of the time, Pallas kernels for 0%

commit v1 on v0

--- a/solution.py
+++ b/solution.py
@@ -19,6 +19,11 @@
         value = combine(value, lax.ppermute(value, axis, pairs))
         bit *= 2
     return value
+
+
+def exchange(value, axis, size, reduce):
+    spread = jnp.broadcast_to(value[None], (size,) + value.shape)
+    return reduce(lax.all_to_all(spread, axis, 0, 0, tiled=False), axis=0)
 
 
 def _max(a, b):
@@ -87,11 +92,11 @@
         row_scale0 = jnp.ones((row_blocks, tile_width), jnp.float32)
         col_scale0 = jnp.ones((col_blocks, tile_width), jnp.float32)
         row_local1 = row_peaks(col_scale0)
-        link_peak1 = butterfly(row_local1[link_start:], "col", n_col, _max)
+        link_peak1 = exchange(row_local1[link_start:], "col", n_col, jnp.max)
         row_scale1 = rescale(row_scale0, jnp.concatenate([row_local1[:link_start], link_peak1], axis=0))
         col_local1 = col_peaks(row_scale0)
         col_local2 = col_peaks(row_scale1)
-        col_both = butterfly(jnp.concatenate([col_local1, col_local2], axis=0), "row", n_row, _max)
+        col_both = exchange(jnp.concatenate([col_local1, col_local2], axis=0), "row", n_row, jnp.max)
         col_scale1 = rescale(col_scale0, col_both[:col_blocks])
         col_scale = rescale(col_scale1, col_both[col_blocks:])
 
@@ -103,7 +108,7 @@
         cost_square = jnp.sum(cost * cost)
         slot = jnp.where(lanes == c, cost_square, 0.0)
         slot = jnp.where(is_period & (lanes == n_col + c // n_row), period_square, slot)
-        packed2 = butterfly(jnp.concatenate([row_local2[link_start:], slot], axis=0), "col", n_col, _max)
+        packed2 = exchange(jnp.concatenate([row_local2[link_start:], slot], axis=0), "col", n_col, jnp.max)
         link_peak2 = packed2[: row_blocks - link_start]
         spare = packed2[row_blocks - link_start]
         cost_total = jnp.sum(spare[:n_col]).reshape(1)
@@ -130,7 +135,7 @@
 
         image0_part = adjoint_local(dual)
         bound_row = jnp.where(lanes == 0, bound_part[0], 0.0)
-        packed3 = butterfly(jnp.concatenate([image0_part, bound_row], axis=0), "row", n_row, _add)
+        packed3 = exchange(jnp.concatenate([image0_part, bound_row], axis=0), "row", n_row, jnp.sum)
         image = packed3[:col_blocks]
         bound_total = packed3[col_blocks, :1]
         weight = jnp.sqrt(cost_total[0] + EPSILON) / jnp.sqrt(bound_total[0] + EPSILON)
@@ -139,13 +144,13 @@
 
         for iteration in range(ITERS):
             if iteration > 0:
-                image = butterfly(adjoint_local(dual), "row", n_row, _add)
+                image = exchange(adjoint_local(dual), "row", n_row, jnp.sum)
             moved = jnp.clip(primal - primal_step * (cost - col_scale * image), low_scaled, high_scaled)
             extra = 2.0 * moved - primal
             partial_rows = forward_local(extra)
             primal = moved
             if iteration < ITERS - 1:
-                link_total = butterfly(partial_rows[link_start:], "col", n_col, _add)
+                link_total = exchange(partial_rows[link_start:], "col", n_col, jnp.sum)
                 total = jnp.concatenate([partial_rows[:link_start], link_total], axis=0)
                 dual = jnp.maximum(dual + dual_step * (bound - row_scale * total), 0.0)
             else:

time: 211 us -> 201 us (0.953)
  starting transfers between devices: 60.2 us -> 35 us
  blocking collectives: 0 us -> 15.3 us
  local copies, waits for them, and re-layouts: 5.8 us -> 9.54 us
  waiting for transfers between devices: 75.1 us -> 72.4 us
    ppermute x29 -> x5, waiting for transfers between devices: 75.1 us -> 20.4 us  [butterfly(): value = combine(value, lax.ppermute(value, axis, pairs))]
    ppermute x29 -> x5, starting transfers between devices: 60.2 us -> 5.56 us  [butterfly(): value = combine(value, lax.ppermute(value, axis, pairs))]
    all_to_all x0 -> x5, waiting for transfers between devices: none -> 52.1 us  [exchange(): return reduce(lax.all_to_all(spread, axis, 0, 0, tiled=False), axis=0)]
    all_to_all x0 -> x5, starting transfers between devices: none -> 29.4 us  [exchange(): return reduce(lax.all_to_all(spread, axis, 0, 0, tiled=False), axis=0)]
    all_to_all x0 -> x1, blocking collectives: none -> 15.3 us  [exchange(): return reduce(lax.all_to_all(spread, axis, 0, 0, tiled=False), axis=0)]
    reduce_max x2 -> x1, other arithmetic: 11.6 us -> 5.77 us  [row_peaks(): row_local = jnp.max(magnitude * col_pieces[:, None, :], axis=2)]
    reduce_max x1 -> x2, other arithmetic: 8.75 us -> 13.8 us  [col_peaks(): col_local = jnp.max(magnitude * row_pieces[:, :, None], axis=1)]
    broadcast_in_dim x0 -> x6, local copies, waits for them, and re-layouts: none -> 3.75 us  [exchange(): spread = jnp.broadcast_to(value[None], (size,) + value.shape)]
  transfers between devices with their start and end apart: 29 -> 10, of which waited for: 29 -> 10; matrix products, arithmetic and copies ran while one was open for 1% -> 1% of each run, Pallas kernels for 0% -> 0%
where the time goes in v1:
time: 201 us; the launch traced here: 200 us
  waiting for transfers between devices  72.4 us (36%)
  starting transfers between devices  35 us (17%)
  other arithmetic  32.2 us (16%)
  matrix products  30.1 us (15%)
  blocking collectives  15.3 us (8%)
  local copies, waits for them, and re-layouts  9.54 us (5%)
  between operations  5.16 us (3%)
    all_to_all x5, waiting for transfers between devices, exchange(): return reduce(lax.all_to_all(spread, axis, 0, 0, tiled=False), axis=0)  52.1 us
    all_to_all x5, starting transfers between devices, exchange(): return reduce(lax.all_to_all(spread, axis, 0, 0, tiled=False), axis=0)  29.4 us
    ppermute x5, waiting for transfers between devices, butterfly(): value = combine(value, lax.ppermute(value, axis, pairs))  20.4 us
    dot_general x2, matrix products, forward_local(): jnp.einsum('tij,tj->ti', matrix, forward_pieces, precision=HIGH)  17.8 us
    all_to_all x1, blocking collectives, exchange(): return reduce(lax.all_to_all(spread, axis, 0, 0, tiled=False), axis=0)  15.3 us
    reduce_max x2, other arithmetic, col_peaks(): col_local = jnp.max(magnitude * row_pieces[:, :, None], axis=1)  13.8 us
    dot_general x2, matrix products, adjoint_local(): products = jnp.einsum('tij,ti->tj', matrix, pieces, precision=HIGH)  11.3 us
    reduce_max x1, other arithmetic, row_peaks(): row_local = jnp.max(magnitude * col_pieces[:, None, :], axis=2)  5.77 us
  transfers between devices with their start and end apart: 10, of which 10 were waited for; matrix products, arithmetic and copies ran while one was open for 1% of the time, Pallas kernels for 0%

profile of v1, /device:TPU:8, one launch (start us, length us, event | category | flops | bytes accessed | tf_op | source)
XLA Modules:
  0.0 199.7 jit_solution(17239420828233558948)
XLA Ops:
  4.3 8.1 %multiply_reduce_fusion.3 = (f32[128,128]{1,0:T(8,128)S(1)}, f32[128,128]{1,0:T(8,128)S(1)}) fusion(f32[1,1,128,128,128]{4,3,2,1,0:T(8,128)} %param.14, f32[128,128]{1,0:T(8,128)S(1)} %get-tuple-element.28, f32[128]{0:T(128)S(1)} %compare_convert_fusion, f32[128,128]{1,0:T(8,128)S(1)} %get-tuple-element.27), kind=kLoop, calls=%fused_computation.25 | loop fusion | flops 12550144 | bytes 8651264 | tf_op jit(solution)/shard_map/reduce_max | solution.py:82
  12.4 1.0 scatter_custom_fusion.1
  14.1 7.5 %all-to-all-start = ((f32[32,16,128]{2,1,0:T(8,128)}), f32[32,16,128]{2,1,0:T(8,128)S(1)}, u32[]{:S(2)}, u32[]{:S(2)}) async-start(f32[32,16,128]{2,1,0:T(8,128)} %broadcast_in_dim.66), calls=%async_computation | async-start | bytes 524288 | tf_op jit(solution)/shard_map/all_to_all | solution.py:26
  21.7 1.0 scatter_custom_fusion
  22.7 6.3 %all-to-all-done = f32[32,16,128]{2,1,0:T(8,128)S(1)} async-done(((f32[32,16,128]{2,1,0:T(8,128)}), f32[32,16,128]{2,1,0:T(8,128)S(1)}, u32[]{:S(2)}, u32[]{:S(2)}) %all-to-all-start) | async-done | bytes 262176 | tf_op jit(solution)/shard_map/all_to_all | solution.py:26
  29.8 5.7 %multiply_reduce_fusion.1 = f32[128,128]{1,0:T(8,128)S(1)} fusion(f32[1,1,128,128,128]{4,3,2,1,0:T(8,128)} %param.14, f32[128,128]{1,0:T(8,128)S(1)} %broadcast_select_fusion.5, f32[128]{0:T(128)S(1)} %compare_convert_fusion), kind=kLoop, calls=%fused_computation.23 | loop fusion | flops 8372224 | bytes 8520192 | tf_op jit(solution)/shard_map/reduce_max | solution.py:82
  35.6 1.0 scatter_custom_fusion.2
  36.6 0.8 broadcast_in_dim.108
  37.4 8.5 %all-to-all-start.1 = ((f32[8,128,128]{2,1,0:T(8,128)}), f32[8,128,128]{2,1,0:T(8,128)S(1)}, u32[]{:S(2)}, u32[]{:S(2)}) async-start(f32[8,128,128]{2,1,0:T(8,128)} %broadcast_in_dim.108), calls=%async_computation.1 | async-start | bytes 1048576 | tf_op jit(solution)/shard_map/all_to_all | solution.py:26
  45.9 18.3 %all-to-all-done.1 = f32[8,128,128]{2,1,0:T(8,128)S(1)} async-done(((f32[8,128,128]{2,1,0:T(8,128)}), f32[8,128,128]{2,1,0:T(8,128)S(1)}, u32[]{:S(2)}, u32[]{:S(2)}) %all-to-all-start.1) | async-done | bytes 524320 | tf_op jit(solution)/shard_map/all_to_all | solution.py:26
  65.6 5.8 %multiply_reduce_fusion = f32[128,128]{1,0:T(8,128)S(1)} fusion(f32[1,1,128,128,128]{4,3,2,1,0:T(8,128)} %param.14, f32[128,128]{1,0:T(8,128)S(1)} %broadcast_select_fusion.4, f32[128]{0:T(128)S(1)} %compare_convert_fusion), kind=kLoop, calls=%fused_computation.22 | loop fusion | flops 8372224 | bytes 8520192 | tf_op jit(solution)/shard_map/reduce_max | solution.py:77
  71.4 1.0 scatter_custom_fusion.3
  73.2 1.3 and_select_fusion
  75.2 5.0 %all-to-all-start.2 = ((f32[32,17,128]{2,1,0:T(8,128)}), f32[32,17,128]{2,1,0:T(8,128)S(1)}, u32[]{:S(2)}, u32[]{:S(2)}) async-start(f32[32,17,128]{2,1,0:T(8,128)} %broadcast_in_dim.113), calls=%async_computation.2 | async-start | bytes 786432 | tf_op jit(solution)/shard_map/all_to_all | solution.py:26
  80.3 8.5 %all-to-all-done.2 = f32[32,17,128]{2,1,0:T(8,128)S(1)} async-done(((f32[32,17,128]{2,1,0:T(8,128)}), f32[32,17,128]{2,1,0:T(8,128)S(1)}, u32[]{:S(2)}, u32[]{:S(2)}) %all-to-all-start.2) | async-done | bytes 278560 | tf_op jit(solution)/shard_map/all_to_all | solution.py:26
  90.4 5.7 %fusion.6 = f32[128,1,128]{2,1,0:T(1,128)S(1)} fusion(f32[128,128,1]{1,2,0:T(1,128)S(1)} %bitcast.154, f32[1,1,128,128,128]{4,3,2,1,0:T(8,128)} %param.14), kind=kOutput, calls=%fused_computation.18 | convolution fusion | flops 12582912 | bytes 8519680 | tf_op jit(solution)/shard_map/tij,ti->tj/dot_general | solution.py:128
  98.9 3.6 %all-to-all-start.3 = ((f32[8,65,128]{2,1,0:T(8,128)}), f32[8,65,128]{2,1,0:T(8,128)S(1)}, u32[]{:S(2)}, u32[]{:S(2)}) async-start(f32[8,65,128]{2,1,0:T(8,128)} %broadcast_in_dim.115), calls=%async_computation.3 | async-start | bytes 589824 | tf_op jit(solution)/shard_map/all_to_all | solution.py:26
  104.5 11.6 %all-to-all-done.3 = f32[8,65,128]{2,1,0:T(8,128)S(1)} async-done(((f32[8,65,128]{2,1,0:T(8,128)}), f32[8,65,128]{2,1,0:T(8,128)S(1)}, u32[]{:S(2)}, u32[]{:S(2)}) %all-to-all-start.3) | async-done | bytes 266272 | tf_op jit(solution)/shard_map/all_to_all | solution.py:26
  118.1 8.9 %fusion.4 = f32[128,1,128]{2,1,0:T(1,128)S(1)} fusion(f32[128,128,1]{1,2,0:T(1,128)S(1)} %bitcast.155, f32[1,1,128,128,128]{4,3,2,1,0:T(8,128)} %param.14), kind=kOutput, calls=%fused_computation.16 | convolution fusion | flops 12582912 | bytes 8519680 | tf_op jit(solution)/shard_map/tij,tj->ti/dot_general | solution.py:133
  128.0 4.8 %all-to-all-start.4 = ((f32[32,16,128]{2,1,0:T(8,128)}), f32[32,16,128]{2,1,0:T(8,128)S(1)}, u32[]{:S(2)}, u32[]{:S(2)}) async-start(f32[32,16,128]{2,1,0:T(8,128)} %broadcast_in_dim.116), calls=%async_computation.4 | async-start | bytes 524288 | tf_op jit(solution)/shard_map/all_to_all | solution.py:26
  132.9 7.3 %all-to-all-done.4 = f32[32,16,128]{2,1,0:T(8,128)S(1)} async-done(((f32[32,16,128]{2,1,0:T(8,128)}), f32[32,16,128]{2,1,0:T(8,128)S(1)}, u32[]{:S(2)}, u32[]{:S(2)}) %all-to-all-start.4) | async-done | bytes 262176 | tf_op jit(solution)/shard_map/all_to_all | solution.py:26
  141.1 5.7 %fusion.2 = f32[128,1,128]{2,1,0:T(1,128)S(1)} fusion(f32[128,128,1]{1,2,0:T(1,128)S(1)} %bitcast.151, f32[1,1,128,128,128]{4,3,2,1,0:T(8,128)} %param.14), kind=kOutput, calls=%fused_computation.14 | convolution fusion | flops 12582912 | bytes 8519680 | tf_op jit(solution)/shard_map/tij,ti->tj/dot_general | solution.py:128
  147.0 15.3 %all_to_all.30 = f32[8,64,128]{2,1,0:T(8,128)S(1)} all-to-all(f32[8,64,128]{2,1,0:T(8,128)S(1)} %broadcast_in_dim.117), channel_id=1, replica_groups=mesh['row'=8,'col'=32] {'row'}, dimensions={0} | all-to-all | bytes 524288 | tf_op jit(solution)/shard_map/all_to_all | solution.py:26
  163.7 8.9 %fusion = f32[128,1,128]{2,1,0:T(1,128)S(1)} fusion(f32[128,128,1]{1,2,0:T(1,128)S(1)} %bitcast.153, f32[1,1,128,128,128]{4,3,2,1,0:T(8,128)} %param.14), kind=kOutput, calls=%fused_computation.12 | convolution fusion | flops 12582912 | bytes 8519680 | tf_op jit(solution)/shard_map/tij,tj->ti/dot_general | solution.py:133
  173.2 1.3 collective-permute-done
  174.5 1.6 collective-permute-start.1
  176.1 4.2 %collective-permute-done.1 = f32[272,128]{1,0:T(8,128)S(1)} collective-permute-done((f32[272,128]{1,0:T(8,128)S(1)}, f32[272,128]{1,0:T(8,128)S(1)}, u32[]{:S(2)}, u32[]{:S(2)}) %collective-permute-start.1) | collective-permute-done | bytes 139296 | tf_op jit(solution)/shard_map/ppermute | solution.py:19
  180.3 1.7 collective-permute-start.2
  182.0 4.9 %collective-permute-done.2 = f32[272,128]{1,0:T(8,128)S(1)} collective-permute-done((f32[272,128]{1,0:T(8,128)S(1)}, f32[272,128]{1,0:T(8,128)S(1)}, u32[]{:S(2)}, u32[]{:S(2)}) %collective-permute-start.2) | collective-permute-done | bytes 139296 | tf_op jit(solution)/shard_map/ppermute | solution.py:19
  187.8 4.6 %collective-permute-done.3 = f32[272,128]{1,0:T(8,128)S(1)} collective-permute-done((f32[272,128]{1,0:T(8,128)S(1)}, f32[272,128]{1,0:T(8,128)S(1)}, u32[]{:S(2)}, u32[]{:S(2)}) %collective-permute-start.3) | collective-permute-done | bytes 139296 | tf_op jit(solution)/shard_map/ppermute | solution.py:19
  192.4 1.3 collective-permute-start.4
  193.6 5.4 %collective-permute-done.4 = f32[272,128]{1,0:T(8,128)S(1)} collective-permute-done((f32[272,128]{1,0:T(8,128)S(1)}, f32[272,128]{1,0:T(8,128)S(1)}, u32[]{:S(2)}, u32[]{:S(2)}) %collective-permute-start.4) | collective-permute-done | bytes 139296 | tf_op jit(solution)/shard_map/ppermute | solution.py:19
  (86 shorter events, 17.9 us)
Async XLA Ops:
  12.3 51.9 %copy-start.2 = (f32[8192]{0:T(1024)S(1)}, f32[8192]{0:T(1024)}, u32[]{:S(2)}) copy-start(f32[8192]{0:T(1024)} %param.17) | copy-start | bytes 98308
  14.1 14.9 %all-to-all-start = ((f32[32,16,128]{2,1,0:T(8,128)}), f32[32,16,128]{2,1,0:T(8,128)S(1)}, u32[]{:S(2)}, u32[]{:S(2)}) async-start(f32[32,16,128]{2,1,0:T(8,128)} %broadcast_in_dim.66), calls=%async_computation | async-start | bytes 524288 | tf_op jit(solution)/shard_map/all_to_all | solution.py:26
  29.8 42.6 %copy-start = (f32[34816]{0:T(1024)S(1)}, f32[34816]{0:T(1024)}, u32[]{:S(2)}) copy-start(f32[34816]{0:T(1024)} %param.20) | copy-start | bytes 417796
  35.6 54.0 %copy-start.1 = (f32[34816]{0:T(1024)S(1)}, f32[34816]{0:T(1024)}, u32[]{:S(2)}) copy-start(f32[34816]{0:T(1024)} %param.22) | copy-start | bytes 417796
  37.4 26.7 %all-to-all-start.1 = ((f32[8,128,128]{2,1,0:T(8,128)}), f32[8,128,128]{2,1,0:T(8,128)S(1)}, u32[]{:S(2)}, u32[]{:S(2)}) async-start(f32[8,128,128]{2,1,0:T(8,128)} %broadcast_in_dim.108), calls=%async_computation.1 | async-start | bytes 1048576 | tf_op jit(solution)/shard_map/all_to_all | solution.py:26
  71.4 46.0 %copy-start.3 = (f32[8192]{0:T(1024)S(1)}, f32[8192]{0:T(1024)}, u32[]{:S(2)}) copy-start(f32[8192]{0:T(1024)} %param.21) | copy-start | bytes 98308
  71.4 46.0 %copy-start.4 = (f32[8192]{0:T(1024)S(1)}, f32[8192]{0:T(1024)}, u32[]{:S(2)}) copy-start(f32[8192]{0:T(1024)} %param.18) | copy-start | bytes 98308
  71.4 46.0 %copy-start.5 = (f32[8192]{0:T(1024)S(1)}, f32[8192]{0:T(1024)}, u32[]{:S(2)}) copy-start(f32[8192]{0:T(1024)} %param.19) | copy-start | bytes 98308
  75.2 13.6 %all-to-all-start.2 = ((f32[32,17,128]{2,1,0:T(8,128)}), f32[32,17,128]{2,1,0:T(8,128)S(1)}, u32[]{:S(2)}, u32[]{:S(2)}) async-start(f32[32,17,128]{2,1,0:T(8,128)} %broadcast_in_dim.113), calls=%async_computation.2 | async-start | bytes 786432 | tf_op jit(solution)/shard_map/all_to_all | solution.py:26
  98.9 17.2 %all-to-all-start.3 = ((f32[8,65,128]{2,1,0:T(8,128)}), f32[8,65,128]{2,1,0:T(8,128)S(1)}, u32[]{:S(2)}, u32[]{:S(2)}) async-start(f32[8,65,128]{2,1,0:T(8,128)} %broadcast_in_dim.115), calls=%async_computation.3 | async-start | bytes 589824 | tf_op jit(solution)/shard_map/all_to_all | solution.py:26
  128.0 12.2 %all-to-all-start.4 = ((f32[32,16,128]{2,1,0:T(8,128)}), f32[32,16,128]{2,1,0:T(8,128)S(1)}, u32[]{:S(2)}, u32[]{:S(2)}) async-start(f32[32,16,128]{2,1,0:T(8,128)} %broadcast_in_dim.116), calls=%async_computation.4 | async-start | bytes 524288 | tf_op jit(solution)/shard_map/all_to_all | solution.py:26
  173.0 1.4 collective-permute-start
  174.5 5.8 %collective-permute-start.1 = (f32[272,128]{1,0:T(8,128)S(1)}, f32[272,128]{1,0:T(8,128)S(1)}, u32[]{:S(2)}, u32[]{:S(2)}) collective-permute-start(f32[272,128]{1,0:T(8,128)S(1)} %fusion.74), channel_id=1, source_target_pairs={{0,2},{1,3},{2,0},{3,1},{4,6},{5,7},{6,4},{7,5},{8,10},{9,11},{10,... | collective-permute-start | bytes 417800 | tf_op jit(solution)/shard_map/ppermute | solution.py:19
  180.3 6.6 %collective-permute-start.2 = (f32[272,128]{1,0:T(8,128)S(1)}, f32[272,128]{1,0:T(8,128)S(1)}, u32[]{:S(2)}, u32[]{:S(2)}) collective-permute-start(f32[272,128]{1,0:T(8,128)S(1)} %add.95), channel_id=1, source_target_pairs={{0,4},{1,5},{2,6},{3,7},{4,0},{5,1},{6,2},{7,3},{8,12},{9,13},{10,... | collective-permute-start | bytes 417800 | tf_op jit(solution)/shard_map/ppermute | solution.py:19
  187.0 5.4 %collective-permute-start.3 = (f32[272,128]{1,0:T(8,128)S(1)}, f32[272,128]{1,0:T(8,128)S(1)}, u32[]{:S(2)}, u32[]{:S(2)}) collective-permute-start(f32[272,128]{1,0:T(8,128)S(1)} %add.96), channel_id=1, source_target_pairs={{0,8},{1,9},{2,10},{3,11},{4,12},{5,13},{6,14},{7,15},{8,0},{9,1},... | collective-permute-start | bytes 417800 | tf_op jit(solution)/shard_map/ppermute | solution.py:19
  192.4 6.6 %collective-permute-start.4 = (f32[272,128]{1,0:T(8,128)S(1)}, f32[272,128]{1,0:T(8,128)S(1)}, u32[]{:S(2)}, u32[]{:S(2)}) collective-permute-start(f32[272,128]{1,0:T(8,128)S(1)} %add.97), channel_id=1, source_target_pairs={{0,16},{1,17},{2,18},{3,19},{4,20},{5,21},{6,22},{7,23},{8,24},{9,... | collective-permute-start | bytes 417800 | tf_op jit(solution)/shard_map/ppermute | solution.py:19

commit v2 on v1

--- a/solution.py
+++ b/solution.py
@@ -96,7 +96,7 @@
         row_scale1 = rescale(row_scale0, jnp.concatenate([row_local1[:link_start], link_peak1], axis=0))
         col_local1 = col_peaks(row_scale0)
         col_local2 = col_peaks(row_scale1)
-        col_both = exchange(jnp.concatenate([col_local1, col_local2], axis=0), "row", n_row, jnp.max)
+        col_both = butterfly(jnp.concatenate([col_local1, col_local2], axis=0), "row", n_row, _max)
         col_scale1 = rescale(col_scale0, col_both[:col_blocks])
         col_scale = rescale(col_scale1, col_both[col_blocks:])
 

time: 201 us -> 198 us (0.985)
  waiting for transfers between devices: 72.4 us -> 63.3 us
  starting transfers between devices: 35 us -> 42 us
    all_to_all x5 -> x4, waiting for transfers between devices: 52.1 us -> 34.1 us  [exchange(): return reduce(lax.all_to_all(spread, axis, 0, 0, tiled=False), axis=0)]
    ppermute x5 -> x8, starting transfers between devices: 5.56 us -> 17 us  [butterfly(): value = combine(value, lax.ppermute(value, axis, pairs))]
    ppermute x5 -> x8, waiting for transfers between devices: 20.4 us -> 29.2 us  [butterfly(): value = combine(value, lax.ppermute(value, axis, pairs))]
    reduce_max x1 -> x2, other arithmetic: 5.77 us -> 11.5 us  [row_peaks(): row_local = jnp.max(magnitude * col_pieces[:, None, :], axis=2)]
    reduce_max x2 -> x1, other arithmetic: 13.8 us -> 8.73 us  [col_peaks(): col_local = jnp.max(magnitude * row_pieces[:, :, None], axis=1)]
    all_to_all x5 -> x4, starting transfers between devices: 29.4 us -> 25 us  [exchange(): return reduce(lax.all_to_all(spread, axis, 0, 0, tiled=False), axis=0)]
  transfers between devices with their start and end apart: 10 -> 12, of which waited for: 10 -> 12; matrix products, arithmetic and copies ran while one was open for 1% -> 1% of each run, Pallas kernels for 0% -> 0%
where the time goes in v2:
time: 198 us; the launch traced here: 197 us
  waiting for transfers between devices  63.3 us (32%)
  starting transfers between devices  42 us (21%)
  other arithmetic  32.9 us (17%)
  matrix products  30.1 us (15%)
  blocking collectives  15.3 us (8%)
  local copies, waits for them, and re-layouts  8.72 us (4%)
  between operations  5.18 us (3%)
    all_to_all x4, waiting for transfers between devices, exchange(): return reduce(lax.all_to_all(spread, axis, 0, 0, tiled=False), axis=0)  34.1 us
    ppermute x8, waiting for transfers between devices, butterfly(): value = combine(value, lax.ppermute(value, axis, pairs))  29.2 us
    all_to_all x4, starting transfers between devices, exchange(): return reduce(lax.all_to_all(spread, axis, 0, 0, tiled=False), axis=0)  25 us
    dot_general x2, matrix products, forward_local(): jnp.einsum('tij,tj->ti', matrix, forward_pieces, precision=HIGH)  17.8 us
    ppermute x8, starting transfers between devices, butterfly(): value = combine(value, lax.ppermute(value, axis, pairs))  17 us
    all_to_all x1, blocking collectives, exchange(): return reduce(lax.all_to_all(spread, axis, 0, 0, tiled=False), axis=0)  15.3 us
    reduce_max x2, other arithmetic, row_peaks(): row_local = jnp.max(magnitude * col_pieces[:, None, :], axis=2)  11.5 us
    dot_general x2, matrix products, adjoint_local(): products = jnp.einsum('tij,ti->tj', matrix, pieces, precision=HIGH)  11.3 us
  transfers between devices with their start and end apart: 12, of which 12 were waited for; matrix products, arithmetic and copies ran while one was open for 1% of the time, Pallas kernels for 0%

profile of v2, /device:TPU:8, one launch (start us, length us, event | category | flops | bytes accessed | tf_op | source)
XLA Modules:
  0.0 197.5 jit_solution(15537979473587713947)
XLA Ops:
  3.6 5.8 %multiply_reduce_fusion.2 = f32[128,128]{1,0:T(8,128)S(1)} fusion(f32[1,1,128,128,128]{4,3,2,1,0:T(8,128)} %param.14, f32[128,128]{1,0:T(8,128)S(1)} %broadcast_select_fusion.6, f32[128]{0:T(128)S(1)} %compare_convert_fusion), kind=kLoop, calls=%fused_computation.24 | loop fusion | flops 8372224 | bytes 8520192 | tf_op jit(solution)/shard_map/reduce_max | solution.py:77
  11.1 7.5 %all-to-all-start = ((f32[32,16,128]{2,1,0:T(8,128)}), f32[32,16,128]{2,1,0:T(8,128)S(1)}, u32[]{:S(2)}, u32[]{:S(2)}) async-start(f32[32,16,128]{2,1,0:T(8,128)} %broadcast_in_dim.101), calls=%async_computation | async-start | bytes 524288 | tf_op jit(solution)/shard_map/all_to_all | solution.py:26
  19.4 6.7 %all-to-all-done = f32[32,16,128]{2,1,0:T(8,128)S(1)} async-done(((f32[32,16,128]{2,1,0:T(8,128)}), f32[32,16,128]{2,1,0:T(8,128)S(1)}, u32[]{:S(2)}, u32[]{:S(2)}) %all-to-all-start) | async-done | bytes 262176 | tf_op jit(solution)/shard_map/all_to_all | solution.py:26
  26.9 8.7 %multiply_reduce_fusion.1 = (f32[128,128]{1,0:T(8,128)S(1)}, f32[128,128]{1,0:T(8,128)S(1)}) fusion(f32[1,1,128,128,128]{4,3,2,1,0:T(8,128)} %param.14, f32[128,128]{1,0:T(8,128)S(1)} %get-tuple-element.26, f32[128]{0:T(128)S(1)} %compare_convert_fusion, f32[128,128]{1,0:T(8,128)S(1)} %get-tuple-element.25), kind=kLoop, calls=%fused_computation.23 | loop fusion | flops 12550144 | bytes 8651264 | tf_op jit(solution)/shard_map/reduce_max | solution.py:82
  35.6 1.0 scatter_custom_fusion.2
  37.7 2.0 %collective-permute-start = (f32[128,128]{1,0:T(8,128)S(1)}, f32[128,128]{1,0:T(8,128)S(1)}, u32[]{:S(2)}, u32[]{:S(2)}) collective-permute-start(f32[128,128]{1,0:T(8,128)S(1)} %constant_dynamic-update-slice_fusion), channel_id=1, source_target_pairs={{0,32},{32,0},{64,96},{96,64},{128,160},{160,128},{192,224},{224,1... | collective-permute-start | bytes 196616 | tf_op jit(solution)/shard_map/ppermute | solution.py:19
  39.7 2.8 %collective-permute-done = f32[128,128]{1,0:T(8,128)S(1)} collective-permute-done((f32[128,128]{1,0:T(8,128)S(1)}, f32[128,128]{1,0:T(8,128)S(1)}, u32[]{:S(2)}, u32[]{:S(2)}) %collective-permute-start) | collective-permute-done | bytes 65568 | tf_op jit(solution)/shard_map/ppermute | solution.py:19
  42.5 3.4 %collective-permute-start.1 = (f32[128,128]{1,0:T(8,128)S(1)}, f32[128,128]{1,0:T(8,128)S(1)}, u32[]{:S(2)}, u32[]{:S(2)}) collective-permute-start(f32[128,128]{1,0:T(8,128)S(1)} %max.36), channel_id=1, source_target_pairs={{0,64},{32,96},{64,0},{96,32},{128,192},{160,224},{192,128},{224,1... | collective-permute-start | bytes 196616 | tf_op jit(solution)/shard_map/ppermute | solution.py:19
  45.9 3.6 %collective-permute-done.1 = f32[128,128]{1,0:T(8,128)S(1)} collective-permute-done((f32[128,128]{1,0:T(8,128)S(1)}, f32[128,128]{1,0:T(8,128)S(1)}, u32[]{:S(2)}, u32[]{:S(2)}) %collective-permute-start.1) | collective-permute-done | bytes 65568 | tf_op jit(solution)/shard_map/ppermute | solution.py:19
  49.6 6.2 %collective-permute-start.2 = (f32[128,128]{1,0:T(8,128)S(1)}, f32[128,128]{1,0:T(8,128)S(1)}, u32[]{:S(2)}, u32[]{:S(2)}) collective-permute-start(f32[128,128]{1,0:T(8,128)S(1)} %max.37), channel_id=1, source_target_pairs={{0,128},{32,160},{64,192},{96,224},{128,0},{160,32},{192,64},{224,... | collective-permute-start | bytes 196616 | tf_op jit(solution)/shard_map/ppermute | solution.py:19
  55.8 2.2 %collective-permute-done.2 = f32[128,128]{1,0:T(8,128)S(1)} collective-permute-done((f32[128,128]{1,0:T(8,128)S(1)}, f32[128,128]{1,0:T(8,128)S(1)}, u32[]{:S(2)}, u32[]{:S(2)}) %collective-permute-start.2) | collective-permute-done | bytes 65568 | tf_op jit(solution)/shard_map/ppermute | solution.py:19
  59.4 5.8 %multiply_reduce_fusion = f32[128,128]{1,0:T(8,128)S(1)} fusion(f32[1,1,128,128,128]{4,3,2,1,0:T(8,128)} %param.14, f32[128,128]{1,0:T(8,128)S(1)} %broadcast_select_fusion.4, f32[128]{0:T(128)S(1)} %compare_convert_fusion), kind=kLoop, calls=%fused_computation.22 | loop fusion | flops 8372224 | bytes 8520192 | tf_op jit(solution)/shard_map/reduce_max | solution.py:77
  66.9 1.3 and_select_fusion
  69.0 5.5 %all-to-all-start.1 = ((f32[32,17,128]{2,1,0:T(8,128)}), f32[32,17,128]{2,1,0:T(8,128)S(1)}, u32[]{:S(2)}, u32[]{:S(2)}) async-start(f32[32,17,128]{2,1,0:T(8,128)} %broadcast_in_dim.106), calls=%async_computation.1 | async-start | bytes 786432 | tf_op jit(solution)/shard_map/all_to_all | solution.py:26
  74.6 8.4 %all-to-all-done.1 = f32[32,17,128]{2,1,0:T(8,128)S(1)} async-done(((f32[32,17,128]{2,1,0:T(8,128)}), f32[32,17,128]{2,1,0:T(8,128)S(1)}, u32[]{:S(2)}, u32[]{:S(2)}) %all-to-all-start.1) | async-done | bytes 278560 | tf_op jit(solution)/shard_map/all_to_all | solution.py:26
  84.5 5.7 %fusion.6 = f32[128,1,128]{2,1,0:T(1,128)S(1)} fusion(f32[128,128,1]{1,2,0:T(1,128)S(1)} %bitcast.154, f32[1,1,128,128,128]{4,3,2,1,0:T(8,128)} %param.14), kind=kOutput, calls=%fused_computation.18 | convolution fusion | flops 12582912 | bytes 8519680 | tf_op jit(solution)/shard_map/tij,ti->tj/dot_general | solution.py:128
  93.1 6.8 %all-to-all-start.2 = ((f32[8,65,128]{2,1,0:T(8,128)}), f32[8,65,128]{2,1,0:T(8,128)S(1)}, u32[]{:S(2)}, u32[]{:S(2)}) async-start(f32[8,65,128]{2,1,0:T(8,128)} %broadcast_in_dim.108), calls=%async_computation.2 | async-start | bytes 589824 | tf_op jit(solution)/shard_map/all_to_all | solution.py:26
  101.8 11.6 %all-to-all-done.2 = f32[8,65,128]{2,1,0:T(8,128)S(1)} async-done(((f32[8,65,128]{2,1,0:T(8,128)}), f32[8,65,128]{2,1,0:T(8,128)S(1)}, u32[]{:S(2)}, u32[]{:S(2)}) %all-to-all-start.2) | async-done | bytes 266272 | tf_op jit(solution)/shard_map/all_to_all | solution.py:26
  115.5 8.9 %fusion.4 = f32[128,1,128]{2,1,0:T(1,128)S(1)} fusion(f32[128,128,1]{1,2,0:T(1,128)S(1)} %bitcast.155, f32[1,1,128,128,128]{4,3,2,1,0:T(8,128)} %param.14), kind=kOutput, calls=%fused_computation.16 | convolution fusion | flops 12582912 | bytes 8519680 | tf_op jit(solution)/shard_map/tij,tj->ti/dot_general | solution.py:133
  125.4 5.1 %all-to-all-start.3 = ((f32[32,16,128]{2,1,0:T(8,128)}), f32[32,16,128]{2,1,0:T(8,128)S(1)}, u32[]{:S(2)}, u32[]{:S(2)}) async-start(f32[32,16,128]{2,1,0:T(8,128)} %broadcast_in_dim.109), calls=%async_computation.3 | async-start | bytes 524288 | tf_op jit(solution)/shard_map/all_to_all | solution.py:26
  130.5 7.4 %all-to-all-done.3 = f32[32,16,128]{2,1,0:T(8,128)S(1)} async-done(((f32[32,16,128]{2,1,0:T(8,128)}), f32[32,16,128]{2,1,0:T(8,128)S(1)}, u32[]{:S(2)}, u32[]{:S(2)}) %all-to-all-start.3) | async-done | bytes 262176 | tf_op jit(solution)/shard_map/all_to_all | solution.py:26
  138.8 5.7 %fusion.2 = f32[128,1,128]{2,1,0:T(1,128)S(1)} fusion(f32[128,128,1]{1,2,0:T(1,128)S(1)} %bitcast.151, f32[1,1,128,128,128]{4,3,2,1,0:T(8,128)} %param.14), kind=kOutput, calls=%fused_computation.14 | convolution fusion | flops 12582912 | bytes 8519680 | tf_op jit(solution)/shard_map/tij,ti->tj/dot_general | solution.py:128
  144.7 15.3 %all_to_all.25 = f32[8,64,128]{2,1,0:T(8,128)S(1)} all-to-all(f32[8,64,128]{2,1,0:T(8,128)S(1)} %broadcast_in_dim.110), channel_id=1, replica_groups=mesh['row'=8,'col'=32] {'row'}, dimensions={0} | all-to-all | bytes 524288 | tf_op jit(solution)/shard_map/all_to_all | solution.py:26
  161.4 8.9 %fusion = f32[128,1,128]{2,1,0:T(1,128)S(1)} fusion(f32[128,128,1]{1,2,0:T(1,128)S(1)} %bitcast.153, f32[1,1,128,128,128]{4,3,2,1,0:T(8,128)} %param.14), kind=kOutput, calls=%fused_computation.12 | convolution fusion | flops 12582912 | bytes 8519680 | tf_op jit(solution)/shard_map/tij,tj->ti/dot_general | solution.py:133
  170.9 1.3 collective-permute-done.3
  172.2 1.6 collective-permute-start.4
  173.8 4.2 %collective-permute-done.4 = f32[272,128]{1,0:T(8,128)S(1)} collective-permute-done((f32[272,128]{1,0:T(8,128)S(1)}, f32[272,128]{1,0:T(8,128)S(1)}, u32[]{:S(2)}, u32[]{:S(2)}) %collective-permute-start.4) | collective-permute-done | bytes 139296 | tf_op jit(solution)/shard_map/ppermute | solution.py:19
  178.0 1.7 collective-permute-start.5
  179.7 4.9 %collective-permute-done.5 = f32[272,128]{1,0:T(8,128)S(1)} collective-permute-done((f32[272,128]{1,0:T(8,128)S(1)}, f32[272,128]{1,0:T(8,128)S(1)}, u32[]{:S(2)}, u32[]{:S(2)}) %collective-permute-start.5) | collective-permute-done | bytes 139296 | tf_op jit(solution)/shard_map/ppermute | solution.py:19
  185.5 4.6 %collective-permute-done.6 = f32[272,128]{1,0:T(8,128)S(1)} collective-permute-done((f32[272,128]{1,0:T(8,128)S(1)}, f32[272,128]{1,0:T(8,128)S(1)}, u32[]{:S(2)}, u32[]{:S(2)}) %collective-permute-start.6) | collective-permute-done | bytes 139296 | tf_op jit(solution)/shard_map/ppermute | solution.py:19
  190.1 1.2 collective-permute-start.7
  191.3 5.4 %collective-permute-done.7 = f32[272,128]{1,0:T(8,128)S(1)} collective-permute-done((f32[272,128]{1,0:T(8,128)S(1)}, f32[272,128]{1,0:T(8,128)S(1)}, u32[]{:S(2)}, u32[]{:S(2)}) %collective-permute-start.7) | collective-permute-done | bytes 139296 | tf_op jit(solution)/shard_map/ppermute | solution.py:19
  (92 shorter events, 20.9 us)
Async XLA Ops:
  9.4 48.7 %copy-start.2 = (f32[8192]{0:T(1024)S(1)}, f32[8192]{0:T(1024)}, u32[]{:S(2)}) copy-start(f32[8192]{0:T(1024)} %param.17) | copy-start | bytes 98308
  11.1 14.9 %all-to-all-start = ((f32[32,16,128]{2,1,0:T(8,128)}), f32[32,16,128]{2,1,0:T(8,128)S(1)}, u32[]{:S(2)}, u32[]{:S(2)}) async-start(f32[32,16,128]{2,1,0:T(8,128)} %broadcast_in_dim.101), calls=%async_computation | async-start | bytes 524288 | tf_op jit(solution)/shard_map/all_to_all | solution.py:26
  26.8 39.4 %copy-start = (f32[34816]{0:T(1024)S(1)}, f32[34816]{0:T(1024)}, u32[]{:S(2)}) copy-start(f32[34816]{0:T(1024)} %param.20) | copy-start | bytes 417796
  35.6 48.1 %copy-start.1 = (f32[34816]{0:T(1024)S(1)}, f32[34816]{0:T(1024)}, u32[]{:S(2)}) copy-start(f32[34816]{0:T(1024)} %param.22) | copy-start | bytes 417796
  37.7 4.8 %collective-permute-start = (f32[128,128]{1,0:T(8,128)S(1)}, f32[128,128]{1,0:T(8,128)S(1)}, u32[]{:S(2)}, u32[]{:S(2)}) collective-permute-start(f32[128,128]{1,0:T(8,128)S(1)} %constant_dynamic-update-slice_fusion), channel_id=1, source_target_pairs={{0,32},{32,0},{64,96},{96,64},{128,160},{160,128},{192,224},{224,1... | collective-permute-start | bytes 196616 | tf_op jit(solution)/shard_map/ppermute | solution.py:19
  42.5 7.0 %collective-permute-start.1 = (f32[128,128]{1,0:T(8,128)S(1)}, f32[128,128]{1,0:T(8,128)S(1)}, u32[]{:S(2)}, u32[]{:S(2)}) collective-permute-start(f32[128,128]{1,0:T(8,128)S(1)} %max.36), channel_id=1, source_target_pairs={{0,64},{32,96},{64,0},{96,32},{128,192},{160,224},{192,128},{224,1... | collective-permute-start | bytes 196616 | tf_op jit(solution)/shard_map/ppermute | solution.py:19
  49.6 8.4 %collective-permute-start.2 = (f32[128,128]{1,0:T(8,128)S(1)}, f32[128,128]{1,0:T(8,128)S(1)}, u32[]{:S(2)}, u32[]{:S(2)}) collective-permute-start(f32[128,128]{1,0:T(8,128)S(1)} %max.37), channel_id=1, source_target_pairs={{0,128},{32,160},{64,192},{96,224},{128,0},{160,32},{192,64},{224,... | collective-permute-start | bytes 196616 | tf_op jit(solution)/shard_map/ppermute | solution.py:19
  65.1 49.5 %copy-start.3 = (f32[8192]{0:T(1024)S(1)}, f32[8192]{0:T(1024)}, u32[]{:S(2)}) copy-start(f32[8192]{0:T(1024)} %param.21) | copy-start | bytes 98308
  65.2 49.5 %copy-start.4 = (f32[8192]{0:T(1024)S(1)}, f32[8192]{0:T(1024)}, u32[]{:S(2)}) copy-start(f32[8192]{0:T(1024)} %param.18) | copy-start | bytes 98308
  65.2 49.5 %copy-start.5 = (f32[8192]{0:T(1024)S(1)}, f32[8192]{0:T(1024)}, u32[]{:S(2)}) copy-start(f32[8192]{0:T(1024)} %param.19) | copy-start | bytes 98308
  69.0 14.0 %all-to-all-start.1 = ((f32[32,17,128]{2,1,0:T(8,128)}), f32[32,17,128]{2,1,0:T(8,128)S(1)}, u32[]{:S(2)}, u32[]{:S(2)}) async-start(f32[32,17,128]{2,1,0:T(8,128)} %broadcast_in_dim.106), calls=%async_computation.1 | async-start | bytes 786432 | tf_op jit(solution)/shard_map/all_to_all | solution.py:26
  93.1 20.3 %all-to-all-start.2 = ((f32[8,65,128]{2,1,0:T(8,128)}), f32[8,65,128]{2,1,0:T(8,128)S(1)}, u32[]{:S(2)}, u32[]{:S(2)}) async-start(f32[8,65,128]{2,1,0:T(8,128)} %broadcast_in_dim.108), calls=%async_computation.2 | async-start | bytes 589824 | tf_op jit(solution)/shard_map/all_to_all | solution.py:26
  125.4 12.6 %all-to-all-start.3 = ((f32[32,16,128]{2,1,0:T(8,128)}), f32[32,16,128]{2,1,0:T(8,128)S(1)}, u32[]{:S(2)}, u32[]{:S(2)}) async-start(f32[32,16,128]{2,1,0:T(8,128)} %broadcast_in_dim.109), calls=%async_computation.3 | async-start | bytes 524288 | tf_op jit(solution)/shard_map/all_to_all | solution.py:26
  170.7 1.4 collective-permute-start.3
  172.2 5.8 %collective-permute-start.4 = (f32[272,128]{1,0:T(8,128)S(1)}, f32[272,128]{1,0:T(8,128)S(1)}, u32[]{:S(2)}, u32[]{:S(2)}) collective-permute-start(f32[272,128]{1,0:T(8,128)S(1)} %fusion.74), channel_id=1, source_target_pairs={{0,2},{1,3},{2,0},{3,1},{4,6},{5,7},{6,4},{7,5},{8,10},{9,11},{10,... | collective-permute-start | bytes 417800 | tf_op jit(solution)/shard_map/ppermute | solution.py:19
  178.0 6.6 %collective-permute-start.5 = (f32[272,128]{1,0:T(8,128)S(1)}, f32[272,128]{1,0:T(8,128)S(1)}, u32[]{:S(2)}, u32[]{:S(2)}) collective-permute-start(f32[272,128]{1,0:T(8,128)S(1)} %add.95), channel_id=1, source_target_pairs={{0,4},{1,5},{2,6},{3,7},{4,0},{5,1},{6,2},{7,3},{8,12},{9,13},{10,... | collective-permute-start | bytes 417800 | tf_op jit(solution)/shard_map/ppermute | solution.py:19
  184.7 5.4 %collective-permute-start.6 = (f32[272,128]{1,0:T(8,128)S(1)}, f32[272,128]{1,0:T(8,128)S(1)}, u32[]{:S(2)}, u32[]{:S(2)}) collective-permute-start(f32[272,128]{1,0:T(8,128)S(1)} %add.96), channel_id=1, source_target_pairs={{0,8},{1,9},{2,10},{3,11},{4,12},{5,13},{6,14},{7,15},{8,0},{9,1},... | collective-permute-start | bytes 417800 | tf_op jit(solution)/shard_map/ppermute | solution.py:19
  190.1 6.6 %collective-permute-start.7 = (f32[272,128]{1,0:T(8,128)S(1)}, f32[272,128]{1,0:T(8,128)S(1)}, u32[]{:S(2)}, u32[]{:S(2)}) collective-permute-start(f32[272,128]{1,0:T(8,128)S(1)} %add.97), channel_id=1, source_target_pairs={{0,16},{1,17},{2,18},{3,19},{4,20},{5,21},{6,22},{7,23},{8,24},{9,... | collective-permute-start | bytes 417800 | tf_op jit(solution)/shard_map/ppermute | solution.py:19

commit v3 on v2

--- a/solution.py
+++ b/solution.py
@@ -130,7 +130,7 @@
 
         def forward_local(extra):
             forward_pieces = jnp.take(col_scale * extra, block_cols, axis=0)
-            forward_products = jnp.einsum("tij,tj->ti", matrix, forward_pieces, precision=HIGH)
+            forward_products = jnp.sum(matrix * forward_pieces[:, None, :], axis=2)
             return jnp.dot(row_onehot, forward_products, precision=HIGHEST)
 
         image0_part = adjoint_local(dual)
@@ -156,12 +156,29 @@
             else:
                 own_dual = jnp.maximum(dual + dual_step * (bound - row_scale * partial_rows), 0.0)
                 own_out = jnp.where(own_period, row_scale * own_dual, 0.0)
-                joined = butterfly(
-                    jnp.concatenate([own_out[:link_start], partial_rows[link_start:]], axis=0),
-                    "col",
-                    n_col,
-                    _add,
-                )
+                segment = lax.dynamic_slice_in_dim(own_out, seg_start, col_blocks, axis=0)
+                carried = jnp.concatenate([segment, partial_rows[link_start:]], axis=0)
+                bit = 1
+                while bit < n_row:
+                    carried = carried + lax.ppermute(carried, "col", [(i, i ^ bit) for i in range(n_col)])
+                    bit *= 2
+                segments = carried[:col_blocks]
+                link_sum = carried[col_blocks:]
+                group = c // n_row
+                while bit < n_col:
+                    held = segments.shape[0]
+                    other = lax.ppermute(
+                        jnp.concatenate([segments, link_sum], axis=0), "col", [(i, i ^ bit) for i in range(n_col)]
+                    )
+                    upper_half = (group & (bit // n_row)) != 0
+                    segments = jnp.where(
+                        upper_half,
+                        jnp.concatenate([other[:held], segments], axis=0),
+                        jnp.concatenate([segments, other[:held]], axis=0),
+                    )
+                    link_sum = link_sum + other[held:]
+                    bit *= 2
+                joined = jnp.concatenate([segments, link_sum], axis=0)
                 link_dual = jnp.maximum(
                     dual[link_start:]
                     + dual_step * (bound[link_start:] - row_scale[link_start:] * joined[link_start:]),

time: 198 us -> 189 us (0.955)
  matrix products: 30.1 us -> 12.2 us
  blocking collectives: 15.3 us -> 0 us
  other arithmetic: 32.9 us -> 44.1 us
  waiting for transfers between devices: 63.3 us -> 71.6 us
  starting transfers between devices: 42 us -> 45 us
    ppermute x8 -> x3, waiting for transfers between devices: 29.2 us -> 8.71 us  [butterfly(): value = combine(value, lax.ppermute(value, axis, pairs))]
    dot_general x2 -> x0, matrix products: 17.8 us -> none  [forward_local(): jnp.einsum('tij,tj->ti', matrix, forward_pieces, precision=HIGH)]
    ppermute x0 -> x5, waiting for transfers between devices: none -> 16.1 us  [the longest x2 8.61 us: local(): lax.ppermute(jnp.concatenate([segments, link_sum], axis=0), 'col', [(i, i...]
    all_to_all x1 -> x0, blocking collectives: 15.3 us -> none  [exchange(): return reduce(lax.all_to_all(spread, axis, 0, 0, tiled=False), axis=0)]
    all_to_all x4 -> x5, waiting for transfers between devices: 34.1 us -> 46.8 us  [exchange(): return reduce(lax.all_to_all(spread, axis, 0, 0, tiled=False), axis=0)]
    reduce_sum x0 -> x2, other arithmetic: none -> 11.2 us  [forward_local(): forward_products = jnp.sum(matrix * forward_pieces[:, None, :], axis=2)]
    ppermute x8 -> x3, starting transfers between devices: 17 us -> 11.5 us  [butterfly(): value = combine(value, lax.ppermute(value, axis, pairs))]
    ppermute x0 -> x5, starting transfers between devices: none -> 5.1 us  [the longest x3 3.33 us: local(): lax.ppermute(carried, 'col', [(i, i ^ bit) for i in range(n_col)])]
  transfers between devices with their start and end apart: 12 -> 13, of which waited for: 12 -> 13; matrix products, arithmetic and copies ran while one was open for 1% -> 1% of each run, Pallas kernels for 0% -> 0%
where the time goes in v3:
time: 189 us; the launch traced here: 188 us
  waiting for transfers between devices  71.6 us (38%)
  starting transfers between devices  45 us (24%)
  other arithmetic  44.1 us (23%)
  matrix products  12.2 us (6%)
  local copies, waits for them, and re-layouts  9.49 us (5%)
  between operations  5.19 us (3%)
    all_to_all x5, waiting for transfers between devices, exchange(): return reduce(lax.all_to_all(spread, axis, 0, 0, tiled=False), axis=0)  46.8 us
    all_to_all x5, starting transfers between devices, exchange(): return reduce(lax.all_to_all(spread, axis, 0, 0, tiled=False), axis=0)  28.4 us
    reduce_max x2, other arithmetic, row_peaks(): row_local = jnp.max(magnitude * col_pieces[:, None, :], axis=2)  11.5 us
    ppermute x3, starting transfers between devices, butterfly(): value = combine(value, lax.ppermute(value, axis, pairs))  11.5 us
    dot_general x2, matrix products, adjoint_local(): products = jnp.einsum('tij,ti->tj', matrix, pieces, precision=HIGH)  11.3 us
    reduce_sum x2, other arithmetic, forward_local(): forward_products = jnp.sum(matrix * forward_pieces[:, None, :], axis=2)  11.2 us
    reduce_max x1, other arithmetic, col_peaks(): col_local = jnp.max(magnitude * row_pieces[:, :, None], axis=1)  8.73 us
    ppermute x3, waiting for transfers between devices, butterfly(): value = combine(value, lax.ppermute(value, axis, pairs))  8.71 us
  transfers between devices with their start and end apart: 13, of which 13 were waited for; matrix products, arithmetic and copies ran while one was open for 1% of the time, Pallas kernels for 0%

profile of v3, /device:TPU:8, one launch (start us, length us, event | category | flops | bytes accessed | tf_op | source)
XLA Modules:
  0.0 187.7 jit_solution(5859721176116438124)
XLA Ops:
  3.6 5.8 %multiply_reduce_fusion.2 = f32[128,128]{1,0:T(8,128)S(1)} fusion(f32[1,1,128,128,128]{4,3,2,1,0:T(8,128)} %param.14, f32[128,128]{1,0:T(8,128)S(1)} %broadcast_select_fusion.6, f32[128]{0:T(128)S(1)} %compare_convert_fusion), kind=kLoop, calls=%fused_computation.24 | loop fusion | flops 8372224 | bytes 8520192 | tf_op jit(solution)/shard_map/reduce_max | solution.py:77
  11.1 7.5 %all-to-all-start = ((f32[32,16,128]{2,1,0:T(8,128)}), f32[32,16,128]{2,1,0:T(8,128)S(1)}, u32[]{:S(2)}, u32[]{:S(2)}) async-start(f32[32,16,128]{2,1,0:T(8,128)} %broadcast_in_dim.64), calls=%async_computation | async-start | bytes 524288 | tf_op jit(solution)/shard_map/all_to_all | solution.py:26
  19.4 6.7 %all-to-all-done = f32[32,16,128]{2,1,0:T(8,128)S(1)} async-done(((f32[32,16,128]{2,1,0:T(8,128)}), f32[32,16,128]{2,1,0:T(8,128)S(1)}, u32[]{:S(2)}, u32[]{:S(2)}) %all-to-all-start) | async-done | bytes 262176 | tf_op jit(solution)/shard_map/all_to_all | solution.py:26
  26.9 8.7 %multiply_reduce_fusion.1 = (f32[128,128]{1,0:T(8,128)S(1)}, f32[128,128]{1,0:T(8,128)S(1)}) fusion(f32[1,1,128,128,128]{4,3,2,1,0:T(8,128)} %param.14, f32[128,128]{1,0:T(8,128)S(1)} %get-tuple-element.26, f32[128]{0:T(128)S(1)} %compare_convert_fusion, f32[128,128]{1,0:T(8,128)S(1)} %get-tuple-element.25), kind=kLoop, calls=%fused_computation.23 | loop fusion | flops 12550144 | bytes 8651264 | tf_op jit(solution)/shard_map/reduce_max | solution.py:82
  37.7 2.0 %collective-permute-start = (f32[128,128]{1,0:T(8,128)S(1)}, f32[128,128]{1,0:T(8,128)S(1)}, u32[]{:S(2)}, u32[]{:S(2)}) collective-permute-start(f32[128,128]{1,0:T(8,128)S(1)} %constant_dynamic-update-slice_fusion), channel_id=1, source_target_pairs={{0,32},{32,0},{64,96},{96,64},{128,160},{160,128},{192,224},{224,1... | collective-permute-start | bytes 196616 | tf_op jit(solution)/shard_map/ppermute | solution.py:19
  39.7 2.8 %collective-permute-done = f32[128,128]{1,0:T(8,128)S(1)} collective-permute-done((f32[128,128]{1,0:T(8,128)S(1)}, f32[128,128]{1,0:T(8,128)S(1)}, u32[]{:S(2)}, u32[]{:S(2)}) %collective-permute-start) | collective-permute-done | bytes 65568 | tf_op jit(solution)/shard_map/ppermute | solution.py:19
  42.5 3.4 %collective-permute-start.1 = (f32[128,128]{1,0:T(8,128)S(1)}, f32[128,128]{1,0:T(8,128)S(1)}, u32[]{:S(2)}, u32[]{:S(2)}) collective-permute-start(f32[128,128]{1,0:T(8,128)S(1)} %max.36), channel_id=1, source_target_pairs={{0,64},{32,96},{64,0},{96,32},{128,192},{160,224},{192,128},{224,1... | collective-permute-start | bytes 196616 | tf_op jit(solution)/shard_map/ppermute | solution.py:19
  45.9 3.6 %collective-permute-done.1 = f32[128,128]{1,0:T(8,128)S(1)} collective-permute-done((f32[128,128]{1,0:T(8,128)S(1)}, f32[128,128]{1,0:T(8,128)S(1)}, u32[]{:S(2)}, u32[]{:S(2)}) %collective-permute-start.1) | collective-permute-done | bytes 65568 | tf_op jit(solution)/shard_map/ppermute | solution.py:19
  49.5 6.2 %collective-permute-start.2 = (f32[128,128]{1,0:T(8,128)S(1)}, f32[128,128]{1,0:T(8,128)S(1)}, u32[]{:S(2)}, u32[]{:S(2)}) collective-permute-start(f32[128,128]{1,0:T(8,128)S(1)} %max.37), channel_id=1, source_target_pairs={{0,128},{32,160},{64,192},{96,224},{128,0},{160,32},{192,64},{224,... | collective-permute-start | bytes 196616 | tf_op jit(solution)/shard_map/ppermute | solution.py:19
  55.7 2.2 %collective-permute-done.2 = f32[128,128]{1,0:T(8,128)S(1)} collective-permute-done((f32[128,128]{1,0:T(8,128)S(1)}, f32[128,128]{1,0:T(8,128)S(1)}, u32[]{:S(2)}, u32[]{:S(2)}) %collective-permute-start.2) | collective-permute-done | bytes 65568 | tf_op jit(solution)/shard_map/ppermute | solution.py:19
  59.4 5.8 %multiply_reduce_fusion = f32[128,128]{1,0:T(8,128)S(1)} fusion(f32[1,1,128,128,128]{4,3,2,1,0:T(8,128)} %param.14, f32[128,128]{1,0:T(8,128)S(1)} %broadcast_select_fusion.4, f32[128]{0:T(128)S(1)} %compare_convert_fusion), kind=kLoop, calls=%fused_computation.22 | loop fusion | flops 8372224 | bytes 8520192 | tf_op jit(solution)/shard_map/reduce_max | solution.py:77
  66.9 1.3 and_select_fusion
  69.0 5.5 %all-to-all-start.1 = ((f32[32,17,128]{2,1,0:T(8,128)}), f32[32,17,128]{2,1,0:T(8,128)S(1)}, u32[]{:S(2)}, u32[]{:S(2)}) async-start(f32[32,17,128]{2,1,0:T(8,128)} %broadcast_in_dim.108), calls=%async_computation.1 | async-start | bytes 786432 | tf_op jit(solution)/shard_map/all_to_all | solution.py:26
  74.6 8.4 %all-to-all-done.1 = f32[32,17,128]{2,1,0:T(8,128)S(1)} async-done(((f32[32,17,128]{2,1,0:T(8,128)}), f32[32,17,128]{2,1,0:T(8,128)S(1)}, u32[]{:S(2)}, u32[]{:S(2)}) %all-to-all-start.1) | async-done | bytes 278560 | tf_op jit(solution)/shard_map/all_to_all | solution.py:26
  84.5 5.7 %fusion.2 = f32[128,1,128]{2,1,0:T(1,128)S(1)} fusion(f32[128,128,1]{1,2,0:T(1,128)S(1)} %bitcast.141, f32[1,1,128,128,128]{4,3,2,1,0:T(8,128)} %param.14), kind=kOutput, calls=%fused_computation.16 | convolution fusion | flops 12582912 | bytes 8519680 | tf_op jit(solution)/shard_map/tij,ti->tj/dot_general | solution.py:128
  93.1 6.8 %all-to-all-start.2 = ((f32[8,65,128]{2,1,0:T(8,128)}), f32[8,65,128]{2,1,0:T(8,128)S(1)}, u32[]{:S(2)}, u32[]{:S(2)}) async-start(f32[8,65,128]{2,1,0:T(8,128)} %broadcast_in_dim.110), calls=%async_computation.2 | async-start | bytes 589824 | tf_op jit(solution)/shard_map/all_to_all | solution.py:26
  101.8 11.6 %all-to-all-done.2 = f32[8,65,128]{2,1,0:T(8,128)S(1)} async-done(((f32[8,65,128]{2,1,0:T(8,128)}), f32[8,65,128]{2,1,0:T(8,128)S(1)}, u32[]{:S(2)}, u32[]{:S(2)}) %all-to-all-start.2) | async-done | bytes 266272 | tf_op jit(solution)/shard_map/all_to_all | solution.py:26
  115.5 5.6 %fusion.5 = f32[128,128]{1,0:T(8,128)S(1)} fusion(f32[1,1,128,128,128]{4,3,2,1,0:T(8,128)} %param.14, f32[128,128]{1,0:T(8,128)S(1)} %broadcast_select_fusion.2), kind=kLoop, calls=%fused_computation.20 | loop fusion | flops 4177920 | bytes 8519680 | tf_op jit(solution)/shard_map/reduce_sum | solution.py:133
  122.1 5.1 %all-to-all-start.3 = ((f32[32,16,128]{2,1,0:T(8,128)}), f32[32,16,128]{2,1,0:T(8,128)S(1)}, u32[]{:S(2)}, u32[]{:S(2)}) async-start(f32[32,16,128]{2,1,0:T(8,128)} %broadcast_in_dim.111), calls=%async_computation.3 | async-start | bytes 524288 | tf_op jit(solution)/shard_map/all_to_all | solution.py:26
  127.2 7.4 %all-to-all-done.3 = f32[32,16,128]{2,1,0:T(8,128)S(1)} async-done(((f32[32,16,128]{2,1,0:T(8,128)}), f32[32,16,128]{2,1,0:T(8,128)S(1)}, u32[]{:S(2)}, u32[]{:S(2)}) %all-to-all-start.3) | async-done | bytes 262176 | tf_op jit(solution)/shard_map/all_to_all | solution.py:26
  135.5 5.7 %fusion = f32[128,1,128]{2,1,0:T(1,128)S(1)} fusion(f32[128,128,1]{1,2,0:T(1,128)S(1)} %bitcast.139, f32[1,1,128,128,128]{4,3,2,1,0:T(8,128)} %param.14), kind=kOutput, calls=%fused_computation.13 | convolution fusion | flops 12582912 | bytes 8519680 | tf_op jit(solution)/shard_map/tij,ti->tj/dot_general | solution.py:128
  142.1 3.4 %all-to-all-start.4 = ((f32[8,64,128]{2,1,0:T(8,128)}), f32[8,64,128]{2,1,0:T(8,128)S(1)}, u32[]{:S(2)}, u32[]{:S(2)}) async-start(f32[8,64,128]{2,1,0:T(8,128)} %broadcast_in_dim.112), calls=%async_computation.4 | async-start | bytes 524288 | tf_op jit(solution)/shard_map/all_to_all | solution.py:26
  145.6 12.7 %all-to-all-done.4 = f32[8,64,128]{2,1,0:T(8,128)S(1)} async-done(((f32[8,64,128]{2,1,0:T(8,128)}), f32[8,64,128]{2,1,0:T(8,128)S(1)}, u32[]{:S(2)}, u32[]{:S(2)}) %all-to-all-start.4) | async-done | bytes 262176 | tf_op jit(solution)/shard_map/all_to_all | solution.py:26
  159.7 5.6 %fusion.6 = f32[128,128]{1,0:T(8,128)S(1)} fusion(f32[1,1,128,128,128]{4,3,2,1,0:T(8,128)} %param.14, f32[128,128]{1,0:T(8,128)S(1)} %broadcast_select_fusion), kind=kLoop, calls=%fused_computation.21 | loop fusion | flops 4177920 | bytes 8519680 | tf_op jit(solution)/shard_map/reduce_sum | solution.py:133
  165.9 1.1 collective-permute-done.3
  167.0 1.5 collective-permute-start.4
  168.5 2.5 %collective-permute-done.4 = f32[80,128]{1,0:T(8,128)S(1)} collective-permute-done((f32[80,128]{1,0:T(8,128)S(1)}, f32[80,128]{1,0:T(8,128)S(1)}, u32[]{:S(2)}, u32[]{:S(2)}) %collective-permute-start.4) | collective-permute-done | bytes 40992 | tf_op jit(solution)/shard_map/ppermute | solution.py:163
  171.0 1.6 collective-permute-start.5
  172.6 3.9 %collective-permute-done.5 = f32[80,128]{1,0:T(8,128)S(1)} collective-permute-done((f32[80,128]{1,0:T(8,128)S(1)}, f32[80,128]{1,0:T(8,128)S(1)}, u32[]{:S(2)}, u32[]{:S(2)}) %collective-permute-start.5) | collective-permute-done | bytes 40992 | tf_op jit(solution)/shard_map/ppermute | solution.py:163
  177.2 3.7 %collective-permute-done.6 = f32[80,128]{1,0:T(8,128)S(1)} collective-permute-done((f32[80,128]{1,0:T(8,128)S(1)}, f32[80,128]{1,0:T(8,128)S(1)}, u32[]{:S(2)}, u32[]{:S(2)}) %collective-permute-start.6) | collective-permute-done | bytes 40992 | tf_op jit(solution)/shard_map/ppermute | solution.py:170
  181.0 1.1 collective-permute-start.7
  182.1 4.9 %collective-permute-done.7 = f32[144,128]{1,0:T(8,128)S(1)} collective-permute-done((f32[144,128]{1,0:T(8,128)S(1)}, f32[144,128]{1,0:T(8,128)S(1)}, u32[]{:S(2)}, u32[]{:S(2)}) %collective-permute-start.7) | collective-permute-done | bytes 73760 | tf_op jit(solution)/shard_map/ppermute | solution.py:170
  (98 shorter events, 22.5 us)
Async XLA Ops:
  9.4 48.6 %copy-start.2 = (f32[8192]{0:T(1024)S(1)}, f32[8192]{0:T(1024)}, u32[]{:S(2)}) copy-start(f32[8192]{0:T(1024)} %param.17) | copy-start | bytes 98308
  11.1 14.9 %all-to-all-start = ((f32[32,16,128]{2,1,0:T(8,128)}), f32[32,16,128]{2,1,0:T(8,128)S(1)}, u32[]{:S(2)}, u32[]{:S(2)}) async-start(f32[32,16,128]{2,1,0:T(8,128)} %broadcast_in_dim.64), calls=%async_computation | async-start | bytes 524288 | tf_op jit(solution)/shard_map/all_to_all | solution.py:26
  26.8 39.4 %copy-start = (f32[34816]{0:T(1024)S(1)}, f32[34816]{0:T(1024)}, u32[]{:S(2)}) copy-start(f32[34816]{0:T(1024)} %param.20) | copy-start | bytes 417796
  35.6 48.1 %copy-start.1 = (f32[34816]{0:T(1024)S(1)}, f32[34816]{0:T(1024)}, u32[]{:S(2)}) copy-start(f32[34816]{0:T(1024)} %param.22) | copy-start | bytes 417796
  37.7 4.8 %collective-permute-start = (f32[128,128]{1,0:T(8,128)S(1)}, f32[128,128]{1,0:T(8,128)S(1)}, u32[]{:S(2)}, u32[]{:S(2)}) collective-permute-start(f32[128,128]{1,0:T(8,128)S(1)} %constant_dynamic-update-slice_fusion), channel_id=1, source_target_pairs={{0,32},{32,0},{64,96},{96,64},{128,160},{160,128},{192,224},{224,1... | collective-permute-start | bytes 196616 | tf_op jit(solution)/shard_map/ppermute | solution.py:19
  42.5 7.0 %collective-permute-start.1 = (f32[128,128]{1,0:T(8,128)S(1)}, f32[128,128]{1,0:T(8,128)S(1)}, u32[]{:S(2)}, u32[]{:S(2)}) collective-permute-start(f32[128,128]{1,0:T(8,128)S(1)} %max.36), channel_id=1, source_target_pairs={{0,64},{32,96},{64,0},{96,32},{128,192},{160,224},{192,128},{224,1... | collective-permute-start | bytes 196616 | tf_op jit(solution)/shard_map/ppermute | solution.py:19
  49.5 8.4 %collective-permute-start.2 = (f32[128,128]{1,0:T(8,128)S(1)}, f32[128,128]{1,0:T(8,128)S(1)}, u32[]{:S(2)}, u32[]{:S(2)}) collective-permute-start(f32[128,128]{1,0:T(8,128)S(1)} %max.37), channel_id=1, source_target_pairs={{0,128},{32,160},{64,192},{96,224},{128,0},{160,32},{192,64},{224,... | collective-permute-start | bytes 196616 | tf_op jit(solution)/shard_map/ppermute | solution.py:19
  65.1 49.5 %copy-start.3 = (f32[8192]{0:T(1024)S(1)}, f32[8192]{0:T(1024)}, u32[]{:S(2)}) copy-start(f32[8192]{0:T(1024)} %param.21) | copy-start | bytes 98308
  65.2 49.5 %copy-start.4 = (f32[8192]{0:T(1024)S(1)}, f32[8192]{0:T(1024)}, u32[]{:S(2)}) copy-start(f32[8192]{0:T(1024)} %param.18) | copy-start | bytes 98308
  65.2 49.5 %copy-start.5 = (f32[8192]{0:T(1024)S(1)}, f32[8192]{0:T(1024)}, u32[]{:S(2)}) copy-start(f32[8192]{0:T(1024)} %param.19) | copy-start | bytes 98308
  69.0 14.0 %all-to-all-start.1 = ((f32[32,17,128]{2,1,0:T(8,128)}), f32[32,17,128]{2,1,0:T(8,128)S(1)}, u32[]{:S(2)}, u32[]{:S(2)}) async-start(f32[32,17,128]{2,1,0:T(8,128)} %broadcast_in_dim.108), calls=%async_computation.1 | async-start | bytes 786432 | tf_op jit(solution)/shard_map/all_to_all | solution.py:26
  93.1 20.3 %all-to-all-start.2 = ((f32[8,65,128]{2,1,0:T(8,128)}), f32[8,65,128]{2,1,0:T(8,128)S(1)}, u32[]{:S(2)}, u32[]{:S(2)}) async-start(f32[8,65,128]{2,1,0:T(8,128)} %broadcast_in_dim.110), calls=%async_computation.2 | async-start | bytes 589824 | tf_op jit(solution)/shard_map/all_to_all | solution.py:26
  122.1 12.6 %all-to-all-start.3 = ((f32[32,16,128]{2,1,0:T(8,128)}), f32[32,16,128]{2,1,0:T(8,128)S(1)}, u32[]{:S(2)}, u32[]{:S(2)}) async-start(f32[32,16,128]{2,1,0:T(8,128)} %broadcast_in_dim.111), calls=%async_computation.3 | async-start | bytes 524288 | tf_op jit(solution)/shard_map/all_to_all | solution.py:26
  142.1 16.2 %all-to-all-start.4 = ((f32[8,64,128]{2,1,0:T(8,128)}), f32[8,64,128]{2,1,0:T(8,128)S(1)}, u32[]{:S(2)}, u32[]{:S(2)}) async-start(f32[8,64,128]{2,1,0:T(8,128)} %broadcast_in_dim.112), calls=%async_computation.4 | async-start | bytes 524288 | tf_op jit(solution)/shard_map/all_to_all | solution.py:26
  165.7 1.3 collective-permute-start.3
  167.0 4.0 %collective-permute-start.4 = (f32[80,128]{1,0:T(8,128)S(1)}, f32[80,128]{1,0:T(8,128)S(1)}, u32[]{:S(2)}, u32[]{:S(2)}) collective-permute-start(f32[80,128]{1,0:T(8,128)S(1)} %fusion.73), channel_id=1, source_target_pairs={{0,2},{1,3},{2,0},{3,1},{4,6},{5,7},{6,4},{7,5},{8,10},{9,11},{10,... | collective-permute-start | bytes 122888 | tf_op jit(solution)/shard_map/ppermute | solution.py:163
  171.0 5.5 %collective-permute-start.5 = (f32[80,128]{1,0:T(8,128)S(1)}, f32[80,128]{1,0:T(8,128)S(1)}, u32[]{:S(2)}, u32[]{:S(2)}) collective-permute-start(f32[80,128]{1,0:T(8,128)S(1)} %add.99), channel_id=1, source_target_pairs={{0,4},{1,5},{2,6},{3,7},{4,0},{5,1},{6,2},{7,3},{8,12},{9,13},{10,... | collective-permute-start | bytes 122888 | tf_op jit(solution)/shard_map/ppermute | solution.py:163
  176.5 4.4 %collective-permute-start.6 = (f32[80,128]{1,0:T(8,128)S(1)}, f32[80,128]{1,0:T(8,128)S(1)}, u32[]{:S(2)}, u32[]{:S(2)}) collective-permute-start(f32[80,128]{1,0:T(8,128)S(1)} %add.100), channel_id=1, source_target_pairs={{0,8},{1,9},{2,10},{3,11},{4,12},{5,13},{6,14},{7,15},{8,0},{9,1},... | collective-permute-start | bytes 122888 | tf_op jit(solution)/shard_map/ppermute | solution.py:170
  181.0 5.9 %collective-permute-start.7 = (f32[144,128]{1,0:T(8,128)S(1)}, f32[144,128]{1,0:T(8,128)S(1)}, u32[]{:S(2)}, u32[]{:S(2)}) collective-permute-start(f32[144,128]{1,0:T(8,128)S(1)} %pad_maximum_fusion), channel_id=1, source_target_pairs={{0,16},{1,17},{2,18},{3,19},{4,20},{5,21},{6,22},{7,23},{8,24},{9,... | collective-permute-start | bytes 221192 | tf_op jit(solution)/shard_map/ppermute | solution.py:170

commit v4 on v3

--- a/solution.py
+++ b/solution.py
@@ -96,9 +96,20 @@
         row_scale1 = rescale(row_scale0, jnp.concatenate([row_local1[:link_start], link_peak1], axis=0))
         col_local1 = col_peaks(row_scale0)
         col_local2 = col_peaks(row_scale1)
-        col_both = butterfly(jnp.concatenate([col_local1, col_local2], axis=0), "row", n_row, _max)
+        first_pieces = jnp.take(dual_start.reshape(row_blocks, tile_width), block_rows, axis=0)
+        first_products = jnp.einsum("tij,ti->tj", matrix, first_pieces, precision=HIGH)
+        image0_part = jnp.dot(col_onehot, first_products, precision=HIGHEST)
+        peak_rows = 2 * col_blocks
+
+        def max_then_add(a, b):
+            return jnp.concatenate([jnp.maximum(a[:peak_rows], b[:peak_rows]), a[peak_rows:] + b[peak_rows:]], axis=0)
+
+        col_both = butterfly(
+            jnp.concatenate([col_local1, col_local2, image0_part], axis=0), "row", n_row, max_then_add
+        )
         col_scale1 = rescale(col_scale0, col_both[:col_blocks])
-        col_scale = rescale(col_scale1, col_both[col_blocks:])
+        col_scale = rescale(col_scale1, col_both[col_blocks:peak_rows])
+        image = col_both[peak_rows:]
 
         row_local2 = row_peaks(col_scale1)
         own_scale2 = rescale(row_scale1, row_local2)
@@ -133,11 +144,8 @@
             forward_products = jnp.sum(matrix * forward_pieces[:, None, :], axis=2)
             return jnp.dot(row_onehot, forward_products, precision=HIGHEST)
 
-        image0_part = adjoint_local(dual)
         bound_row = jnp.where(lanes == 0, bound_part[0], 0.0)
-        packed3 = exchange(jnp.concatenate([image0_part, bound_row], axis=0), "row", n_row, jnp.sum)
-        image = packed3[:col_blocks]
-        bound_total = packed3[col_blocks, :1]
+        bound_total = exchange(bound_row, "row", n_row, jnp.sum)[0, :1]
         weight = jnp.sqrt(cost_total[0] + EPSILON) / jnp.sqrt(bound_total[0] + EPSILON)
         primal_step = step_size[0] / weight
         dual_step = step_size[0] * weight

time: 189 us -> 182 us (0.963)
  waiting for transfers between devices: 71.6 us -> 67.1 us
    all_to_all x5, waiting for transfers between devices: 46.8 us -> 39.8 us  [exchange(): return reduce(lax.all_to_all(spread, axis, 0, 0, tiled=False), axis=0)]
    dot_general x0 -> x2, matrix products: none -> 5.89 us  [the longest x1 5.71 us: local(): jnp.einsum('tij,ti->tj', matrix, first_pieces, precision=HIGH)]
    reduce_max x2 -> x1, other arithmetic: 11.5 us -> 5.77 us  [row_peaks(): row_local = jnp.max(magnitude * col_pieces[:, None, :], axis=2)]
    dot_general x2 -> x1, matrix products: 11.3 us -> 5.67 us  [adjoint_local(): products = jnp.einsum('tij,ti->tj', matrix, pieces, precision=HIGH)]
    reduce_max x1 -> x2, other arithmetic: 8.73 us -> 13.8 us  [col_peaks(): col_local = jnp.max(magnitude * row_pieces[:, :, None], axis=1)]
    ppermute x3, waiting for transfers between devices: 8.71 us -> 11.1 us  [butterfly(): value = combine(value, lax.ppermute(value, axis, pairs))]
where the time goes in v4:
time: 182 us
  waiting for transfers between devices  67.1 us (37%)
  starting transfers between devices  45.3 us (25%)
  other arithmetic  43.4 us (24%)
  matrix products  12.3 us (7%)
  local copies, waits for them, and re-layouts  8.83 us (5%)
  between operations  4.65 us (3%)
    all_to_all x5, waiting for transfers between devices, exchange(): return reduce(lax.all_to_all(spread, axis, 0, 0, tiled=False), axis=0)  39.8 us
    all_to_all x5, starting transfers between devices, exchange(): return reduce(lax.all_to_all(spread, axis, 0, 0, tiled=False), axis=0)  28.5 us
    reduce_max x2, other arithmetic, col_peaks(): col_local = jnp.max(magnitude * row_pieces[:, :, None], axis=1)  13.8 us
    ppermute x3, starting transfers between devices, butterfly(): value = combine(value, lax.ppermute(value, axis, pairs))  11.7 us
    reduce_sum x2, other arithmetic, forward_local(): forward_products = jnp.sum(matrix * forward_pieces[:, None, :], axis=2)  11.2 us
    ppermute x3, waiting for transfers between devices, butterfly(): value = combine(value, lax.ppermute(value, axis, pairs))  11.1 us
    ppermute x2, waiting for transfers between devices, local(): lax.ppermute(jnp.concatenate([segments, link_sum], axis=0), 'col', [(i, i...  8.62 us
    ppermute x3, waiting for transfers between devices, local(): lax.ppermute(carried, 'col', [(i, i ^ bit) for i in range(n_col)])  7.51 us
  transfers between devices with their start and end apart: 13, of which 13 were waited for; matrix products, arithmetic and copies ran while one was open for 1% of the time, Pallas kernels for 0%

profile of v4, /device:TPU:8, one launch (start us, length us, event | category | flops | bytes accessed | tf_op | source)
XLA Modules:
  0.0 181.5 jit_solution(2266499745520596286)
XLA Ops:
  4.3 8.1 %multiply_reduce_fusion.3 = (f32[128,128]{1,0:T(8,128)S(1)}, f32[128,128]{1,0:T(8,128)S(1)}) fusion(f32[1,1,128,128,128]{4,3,2,1,0:T(8,128)} %param.14, f32[128,128]{1,0:T(8,128)S(1)} %get-tuple-element.32, f32[128]{0:T(128)S(1)} %compare_convert_fusion, f32[128,128]{1,0:T(8,128)S(1)} %get-tuple-element.31), kind=kLoop, calls=%fused_computation.25 | loop fusion | flops 12550144 | bytes 8651264 | tf_op jit(solution)/shard_map/reduce_max | solution.py:82
  14.1 7.5 %all-to-all-start = ((f32[32,16,128]{2,1,0:T(8,128)}), f32[32,16,128]{2,1,0:T(8,128)S(1)}, u32[]{:S(2)}, u32[]{:S(2)}) async-start(f32[32,16,128]{2,1,0:T(8,128)} %broadcast_in_dim.105), calls=%async_computation | async-start | bytes 524288 | tf_op jit(solution)/shard_map/all_to_all | solution.py:26
  23.4 5.7 %all-to-all-done = f32[32,16,128]{2,1,0:T(8,128)S(1)} async-done(((f32[32,16,128]{2,1,0:T(8,128)}), f32[32,16,128]{2,1,0:T(8,128)S(1)}, u32[]{:S(2)}, u32[]{:S(2)}) %all-to-all-start) | async-done | bytes 262176 | tf_op jit(solution)/shard_map/all_to_all | solution.py:26
  29.8 5.7 %multiply_reduce_fusion.1 = f32[128,128]{1,0:T(8,128)S(1)} fusion(f32[1,1,128,128,128]{4,3,2,1,0:T(8,128)} %param.14, f32[128,128]{1,0:T(8,128)S(1)} %get-tuple-element.27, f32[128]{0:T(128)S(1)} %compare_convert_fusion), kind=kLoop, calls=%fused_computation.23 | loop fusion | flops 8372224 | bytes 8520192 | tf_op jit(solution)/shard_map/reduce_max | solution.py:82
  36.6 5.7 %fusion.2 = f32[128,1,128]{2,1,0:T(1,128)S(1)} fusion(f32[128,128,1]{1,2,0:T(1,128)S(1)} %bitcast.121, f32[1,1,128,128,128]{4,3,2,1,0:T(8,128)} %param.14), kind=kOutput, calls=%fused_computation.16 | convolution fusion | flops 12582912 | bytes 8519680 | tf_op jit(solution)/shard_map/tij,ti->tj/dot_general | solution.py:100
  42.5 2.0 %collective-permute-start = (f32[192,128]{1,0:T(8,128)S(1)}, f32[192,128]{1,0:T(8,128)S(1)}, u32[]{:S(2)}, u32[]{:S(2)}) collective-permute-start(f32[192,128]{1,0:T(8,128)S(1)} %pad_maximum_fusion), channel_id=1, source_target_pairs={{0,32},{32,0},{64,96},{96,64},{128,160},{160,128},{192,224},{224,1... | collective-permute-start | bytes 294920 | tf_op jit(solution)/shard_map/ppermute | solution.py:19
  44.5 3.5 %collective-permute-done = f32[192,128]{1,0:T(8,128)S(1)} collective-permute-done((f32[192,128]{1,0:T(8,128)S(1)}, f32[192,128]{1,0:T(8,128)S(1)}, u32[]{:S(2)}, u32[]{:S(2)}) %collective-permute-start) | collective-permute-done | bytes 98336 | tf_op jit(solution)/shard_map/ppermute | solution.py:19
  48.1 3.4 %collective-permute-start.1 = (f32[192,128]{1,0:T(8,128)S(1)}, f32[192,128]{1,0:T(8,128)S(1)}, u32[]{:S(2)}, u32[]{:S(2)}) collective-permute-start(f32[192,128]{1,0:T(8,128)S(1)} %pad_maximum_fusion.1), channel_id=1, source_target_pairs={{0,64},{32,96},{64,0},{96,32},{128,192},{160,224},{192,128},{224,1... | collective-permute-start | bytes 294920 | tf_op jit(solution)/shard_map/ppermute | solution.py:19
  51.4 5.0 %collective-permute-done.1 = f32[192,128]{1,0:T(8,128)S(1)} collective-permute-done((f32[192,128]{1,0:T(8,128)S(1)}, f32[192,128]{1,0:T(8,128)S(1)}, u32[]{:S(2)}, u32[]{:S(2)}) %collective-permute-start.1) | collective-permute-done | bytes 98336 | tf_op jit(solution)/shard_map/ppermute | solution.py:19
  56.4 6.3 %collective-permute-start.2 = (f32[192,128]{1,0:T(8,128)S(1)}, f32[192,128]{1,0:T(8,128)S(1)}, u32[]{:S(2)}, u32[]{:S(2)}) collective-permute-start(f32[192,128]{1,0:T(8,128)S(1)} %pad_maximum_fusion.2), channel_id=1, source_target_pairs={{0,128},{32,160},{64,192},{96,224},{128,0},{160,32},{192,64},{224,... | collective-permute-start | bytes 294920 | tf_op jit(solution)/shard_map/ppermute | solution.py:19
  62.7 2.6 %collective-permute-done.2 = f32[192,128]{1,0:T(8,128)S(1)} collective-permute-done((f32[192,128]{1,0:T(8,128)S(1)}, f32[192,128]{1,0:T(8,128)S(1)}, u32[]{:S(2)}, u32[]{:S(2)}) %collective-permute-start.2) | collective-permute-done | bytes 98336 | tf_op jit(solution)/shard_map/ppermute | solution.py:19
  66.7 5.8 %multiply_reduce_fusion = f32[128,128]{1,0:T(8,128)S(1)} fusion(f32[1,1,128,128,128]{4,3,2,1,0:T(8,128)} %param.14, f32[128,128]{1,0:T(8,128)S(1)} %broadcast_select_fusion.3, f32[128]{0:T(128)S(1)} %compare_convert_fusion), kind=kLoop, calls=%fused_computation.22 | loop fusion | flops 8372224 | bytes 8520192 | tf_op jit(solution)/shard_map/reduce_max | solution.py:77
  74.3 1.3 and_select_fusion
  76.4 4.8 %all-to-all-start.1 = ((f32[32,17,128]{2,1,0:T(8,128)}), f32[32,17,128]{2,1,0:T(8,128)S(1)}, u32[]{:S(2)}, u32[]{:S(2)}) async-start(f32[32,17,128]{2,1,0:T(8,128)} %broadcast_in_dim.110), calls=%async_computation.1 | async-start | bytes 786432 | tf_op jit(solution)/shard_map/all_to_all | solution.py:26
  81.9 7.9 %all-to-all-done.1 = f32[32,17,128]{2,1,0:T(8,128)S(1)} async-done(((f32[32,17,128]{2,1,0:T(8,128)}), f32[32,17,128]{2,1,0:T(8,128)S(1)}, u32[]{:S(2)}, u32[]{:S(2)}) %all-to-all-start.1) | async-done | bytes 278560 | tf_op jit(solution)/shard_map/all_to_all | solution.py:26
  93.1 7.4 %all-to-all-start.2 = ((f32[8,1,128]{2,1,0:T(1,128)}), f32[8,1,128]{2,1,0:T(1,128)S(1)}, u32[]{:S(2)}, u32[]{:S(2)}) async-start(f32[8,1,128]{2,1,0:T(1,128)} %broadcast_in_dim.113), calls=%async_computation.2 | async-start | bytes 8192 | tf_op jit(solution)/shard_map/all_to_all | solution.py:26
  102.0 6.2 %all-to-all-done.2 = f32[8,1,128]{2,1,0:T(1,128)S(1)} async-done(((f32[8,1,128]{2,1,0:T(1,128)}), f32[8,1,128]{2,1,0:T(1,128)S(1)}, u32[]{:S(2)}, u32[]{:S(2)}) %all-to-all-start.2) | async-done | bytes 4128 | tf_op jit(solution)/shard_map/all_to_all | solution.py:26
  109.1 5.6 %fusion.5 = f32[128,128]{1,0:T(8,128)S(1)} fusion(f32[1,1,128,128,128]{4,3,2,1,0:T(8,128)} %param.14, f32[128,128]{1,0:T(8,128)S(1)} %broadcast_select_fusion.2), kind=kLoop, calls=%fused_computation.20 | loop fusion | flops 4177920 | bytes 8519680 | tf_op jit(solution)/shard_map/reduce_sum | solution.py:144
  115.8 5.4 %all-to-all-start.3 = ((f32[32,16,128]{2,1,0:T(8,128)}), f32[32,16,128]{2,1,0:T(8,128)S(1)}, u32[]{:S(2)}, u32[]{:S(2)}) async-start(f32[32,16,128]{2,1,0:T(8,128)} %broadcast_in_dim.114), calls=%async_computation.3 | async-start | bytes 524288 | tf_op jit(solution)/shard_map/all_to_all | solution.py:26
  121.2 7.4 %all-to-all-done.3 = f32[32,16,128]{2,1,0:T(8,128)S(1)} async-done(((f32[32,16,128]{2,1,0:T(8,128)}), f32[32,16,128]{2,1,0:T(8,128)S(1)}, u32[]{:S(2)}, u32[]{:S(2)}) %all-to-all-start.3) | async-done | bytes 262176 | tf_op jit(solution)/shard_map/all_to_all | solution.py:26
  129.4 5.7 %fusion = f32[128,1,128]{2,1,0:T(1,128)S(1)} fusion(f32[128,128,1]{1,2,0:T(1,128)S(1)} %bitcast.118, f32[1,1,128,128,128]{4,3,2,1,0:T(8,128)} %param.14), kind=kOutput, calls=%fused_computation.13 | convolution fusion | flops 12582912 | bytes 8519680 | tf_op jit(solution)/shard_map/tij,ti->tj/dot_general | solution.py:139
  135.9 3.4 %all-to-all-start.4 = ((f32[8,64,128]{2,1,0:T(8,128)}), f32[8,64,128]{2,1,0:T(8,128)S(1)}, u32[]{:S(2)}, u32[]{:S(2)}) async-start(f32[8,64,128]{2,1,0:T(8,128)} %broadcast_in_dim.115), calls=%async_computation.4 | async-start | bytes 524288 | tf_op jit(solution)/shard_map/all_to_all | solution.py:26
  139.4 12.7 %all-to-all-done.4 = f32[8,64,128]{2,1,0:T(8,128)S(1)} async-done(((f32[8,64,128]{2,1,0:T(8,128)}), f32[8,64,128]{2,1,0:T(8,128)S(1)}, u32[]{:S(2)}, u32[]{:S(2)}) %all-to-all-start.4) | async-done | bytes 262176 | tf_op jit(solution)/shard_map/all_to_all | solution.py:26
  153.6 5.6 %fusion.6 = f32[128,128]{1,0:T(8,128)S(1)} fusion(f32[1,1,128,128,128]{4,3,2,1,0:T(8,128)} %param.14, f32[128,128]{1,0:T(8,128)S(1)} %broadcast_select_fusion), kind=kLoop, calls=%fused_computation.21 | loop fusion | flops 4177920 | bytes 8519680 | tf_op jit(solution)/shard_map/reduce_sum | solution.py:144
  159.7 1.1 collective-permute-done.3
  160.9 1.5 collective-permute-start.4
  162.4 2.5 %collective-permute-done.4 = f32[80,128]{1,0:T(8,128)S(1)} collective-permute-done((f32[80,128]{1,0:T(8,128)S(1)}, f32[80,128]{1,0:T(8,128)S(1)}, u32[]{:S(2)}, u32[]{:S(2)}) %collective-permute-start.4) | collective-permute-done | bytes 40992 | tf_op jit(solution)/shard_map/ppermute | solution.py:171
  164.9 1.6 collective-permute-start.5
  166.5 3.9 %collective-permute-done.5 = f32[80,128]{1,0:T(8,128)S(1)} collective-permute-done((f32[80,128]{1,0:T(8,128)S(1)}, f32[80,128]{1,0:T(8,128)S(1)}, u32[]{:S(2)}, u32[]{:S(2)}) %collective-permute-start.5) | collective-permute-done | bytes 40992 | tf_op jit(solution)/shard_map/ppermute | solution.py:171
  171.1 3.7 %collective-permute-done.6 = f32[80,128]{1,0:T(8,128)S(1)} collective-permute-done((f32[80,128]{1,0:T(8,128)S(1)}, f32[80,128]{1,0:T(8,128)S(1)}, u32[]{:S(2)}, u32[]{:S(2)}) %collective-permute-start.6) | collective-permute-done | bytes 40992 | tf_op jit(solution)/shard_map/ppermute | solution.py:178
  174.9 1.1 collective-permute-start.7
  175.9 4.9 %collective-permute-done.7 = f32[144,128]{1,0:T(8,128)S(1)} collective-permute-done((f32[144,128]{1,0:T(8,128)S(1)}, f32[144,128]{1,0:T(8,128)S(1)}, u32[]{:S(2)}, u32[]{:S(2)}) %collective-permute-start.7) | collective-permute-done | bytes 73760 | tf_op jit(solution)/shard_map/ppermute | solution.py:178
  (97 shorter events, 22.0 us)
Async XLA Ops:
  0.6 21.0 %copy-start = (f32[34816]{0:T(1024)S(1)}, f32[34816]{0:T(1024)}, u32[]{:S(2)}) copy-start(f32[34816]{0:T(1024)} %param.22) | copy-start | bytes 417796
  14.1 14.9 %all-to-all-start = ((f32[32,16,128]{2,1,0:T(8,128)}), f32[32,16,128]{2,1,0:T(8,128)S(1)}, u32[]{:S(2)}, u32[]{:S(2)}) async-start(f32[32,16,128]{2,1,0:T(8,128)} %broadcast_in_dim.105), calls=%async_computation | async-start | bytes 524288 | tf_op jit(solution)/shard_map/all_to_all | solution.py:26
  29.8 35.5 %copy-start.2 = (f32[8192]{0:T(1024)S(1)}, f32[8192]{0:T(1024)}, u32[]{:S(2)}) copy-start(f32[8192]{0:T(1024)} %param.17) | copy-start | bytes 98308
  36.6 37.0 %copy-start.1 = (f32[34816]{0:T(1024)S(1)}, f32[34816]{0:T(1024)}, u32[]{:S(2)}) copy-start(f32[34816]{0:T(1024)} %param.20) | copy-start | bytes 417796
  42.3 66.1 %copy-start.3 = (f32[8192]{0:T(1024)S(1)}, f32[8192]{0:T(1024)}, u32[]{:S(2)}) copy-start(f32[8192]{0:T(1024)} %param.18) | copy-start | bytes 98308
  42.3 66.1 %copy-start.4 = (f32[8192]{0:T(1024)S(1)}, f32[8192]{0:T(1024)}, u32[]{:S(2)}) copy-start(f32[8192]{0:T(1024)} %param.19) | copy-start | bytes 98308
  42.3 66.1 %copy-start.5 = (f32[8192]{0:T(1024)S(1)}, f32[8192]{0:T(1024)}, u32[]{:S(2)}) copy-start(f32[8192]{0:T(1024)} %param.21) | copy-start | bytes 98308
  42.5 5.5 %collective-permute-start = (f32[192,128]{1,0:T(8,128)S(1)}, f32[192,128]{1,0:T(8,128)S(1)}, u32[]{:S(2)}, u32[]{:S(2)}) collective-permute-start(f32[192,128]{1,0:T(8,128)S(1)} %pad_maximum_fusion), channel_id=1, source_target_pairs={{0,32},{32,0},{64,96},{96,64},{128,160},{160,128},{192,224},{224,1... | collective-permute-start | bytes 294920 | tf_op jit(solution)/shard_map/ppermute | solution.py:19
  48.1 8.3 %collective-permute-start.1 = (f32[192,128]{1,0:T(8,128)S(1)}, f32[192,128]{1,0:T(8,128)S(1)}, u32[]{:S(2)}, u32[]{:S(2)}) collective-permute-start(f32[192,128]{1,0:T(8,128)S(1)} %pad_maximum_fusion.1), channel_id=1, source_target_pairs={{0,64},{32,96},{64,0},{96,32},{128,192},{160,224},{192,128},{224,1... | collective-permute-start | bytes 294920 | tf_op jit(solution)/shard_map/ppermute | solution.py:19
  56.4 8.9 %collective-permute-start.2 = (f32[192,128]{1,0:T(8,128)S(1)}, f32[192,128]{1,0:T(8,128)S(1)}, u32[]{:S(2)}, u32[]{:S(2)}) collective-permute-start(f32[192,128]{1,0:T(8,128)S(1)} %pad_maximum_fusion.2), channel_id=1, source_target_pairs={{0,128},{32,160},{64,192},{96,224},{128,0},{160,32},{192,64},{224,... | collective-permute-start | bytes 294920 | tf_op jit(solution)/shard_map/ppermute | solution.py:19
  76.4 13.4 %all-to-all-start.1 = ((f32[32,17,128]{2,1,0:T(8,128)}), f32[32,17,128]{2,1,0:T(8,128)S(1)}, u32[]{:S(2)}, u32[]{:S(2)}) async-start(f32[32,17,128]{2,1,0:T(8,128)} %broadcast_in_dim.110), calls=%async_computation.1 | async-start | bytes 786432 | tf_op jit(solution)/shard_map/all_to_all | solution.py:26
  93.1 15.1 %all-to-all-start.2 = ((f32[8,1,128]{2,1,0:T(1,128)}), f32[8,1,128]{2,1,0:T(1,128)S(1)}, u32[]{:S(2)}, u32[]{:S(2)}) async-start(f32[8,1,128]{2,1,0:T(1,128)} %broadcast_in_dim.113), calls=%async_computation.2 | async-start | bytes 8192 | tf_op jit(solution)/shard_map/all_to_all | solution.py:26
  115.8 12.8 %all-to-all-start.3 = ((f32[32,16,128]{2,1,0:T(8,128)}), f32[32,16,128]{2,1,0:T(8,128)S(1)}, u32[]{:S(2)}, u32[]{:S(2)}) async-start(f32[32,16,128]{2,1,0:T(8,128)} %broadcast_in_dim.114), calls=%async_computation.3 | async-start | bytes 524288 | tf_op jit(solution)/shard_map/all_to_all | solution.py:26
  135.9 16.2 %all-to-all-start.4 = ((f32[8,64,128]{2,1,0:T(8,128)}), f32[8,64,128]{2,1,0:T(8,128)S(1)}, u32[]{:S(2)}, u32[]{:S(2)}) async-start(f32[8,64,128]{2,1,0:T(8,128)} %broadcast_in_dim.115), calls=%async_computation.4 | async-start | bytes 524288 | tf_op jit(solution)/shard_map/all_to_all | solution.py:26
  159.6 1.3 collective-permute-start.3
  160.9 4.0 %collective-permute-start.4 = (f32[80,128]{1,0:T(8,128)S(1)}, f32[80,128]{1,0:T(8,128)S(1)}, u32[]{:S(2)}, u32[]{:S(2)}) collective-permute-start(f32[80,128]{1,0:T(8,128)S(1)} %fusion.73), channel_id=1, source_target_pairs={{0,2},{1,3},{2,0},{3,1},{4,6},{5,7},{6,4},{7,5},{8,10},{9,11},{10,... | collective-permute-start | bytes 122888 | tf_op jit(solution)/shard_map/ppermute | solution.py:171
  164.9 5.5 %collective-permute-start.5 = (f32[80,128]{1,0:T(8,128)S(1)}, f32[80,128]{1,0:T(8,128)S(1)}, u32[]{:S(2)}, u32[]{:S(2)}) collective-permute-start(f32[80,128]{1,0:T(8,128)S(1)} %add.111), channel_id=1, source_target_pairs={{0,4},{1,5},{2,6},{3,7},{4,0},{5,1},{6,2},{7,3},{8,12},{9,13},{10,... | collective-permute-start | bytes 122888 | tf_op jit(solution)/shard_map/ppermute | solution.py:171
  170.4 4.4 %collective-permute-start.6 = (f32[80,128]{1,0:T(8,128)S(1)}, f32[80,128]{1,0:T(8,128)S(1)}, u32[]{:S(2)}, u32[]{:S(2)}) collective-permute-start(f32[80,128]{1,0:T(8,128)S(1)} %add.112), channel_id=1, source_target_pairs={{0,8},{1,9},{2,10},{3,11},{4,12},{5,13},{6,14},{7,15},{8,0},{9,1},... | collective-permute-start | bytes 122888 | tf_op jit(solution)/shard_map/ppermute | solution.py:178
  174.9 5.9 %collective-permute-start.7 = (f32[144,128]{1,0:T(8,128)S(1)}, f32[144,128]{1,0:T(8,128)S(1)}, u32[]{:S(2)}, u32[]{:S(2)}) collective-permute-start(f32[144,128]{1,0:T(8,128)S(1)} %pad_maximum_fusion.3), channel_id=1, source_target_pairs={{0,16},{1,17},{2,18},{3,19},{4,20},{5,21},{6,22},{7,23},{8,24},{9,... | collective-permute-start | bytes 221192 | tf_op jit(solution)/shard_map/ppermute | solution.py:178

commit v5 on v4

--- a/solution.py
+++ b/solution.py
@@ -97,7 +97,7 @@
         col_local1 = col_peaks(row_scale0)
         col_local2 = col_peaks(row_scale1)
         first_pieces = jnp.take(dual_start.reshape(row_blocks, tile_width), block_rows, axis=0)
-        first_products = jnp.einsum("tij,ti->tj", matrix, first_pieces, precision=HIGH)
+        first_products = jnp.sum(matrix * first_pieces[:, :, None], axis=1)
         image0_part = jnp.dot(col_onehot, first_products, precision=HIGHEST)
         peak_rows = 2 * col_blocks
 

time: 182 us -> 180 us (0.989)
  matrix products: 12.3 us -> 6.58 us
  other arithmetic: 43.4 us -> 45.4 us
    dot_general x1 -> x0, matrix products: 5.71 us -> none  [local(): jnp.einsum('tij,ti->tj', matrix, first_pieces, precision=HIGH)]
    reduce_max x2, other arithmetic: 13.8 us -> 15.7 us  [col_peaks(): col_local = jnp.max(magnitude * row_pieces[:, :, None], axis=1)]
where the time goes in v5:
time: 180 us; the launch traced here: 179 us
  waiting for transfers between devices  67.5 us (38%)
  other arithmetic  45.4 us (25%)
  starting transfers between devices  45.3 us (25%)
  local copies, waits for them, and re-layouts  9.74 us (5%)
  matrix products  6.58 us (4%)
  between operations  4.65 us (3%)
    all_to_all x5, waiting for transfers between devices, exchange(): return reduce(lax.all_to_all(spread, axis, 0, 0, tiled=False), axis=0)  40.3 us
    all_to_all x5, starting transfers between devices, exchange(): return reduce(lax.all_to_all(spread, axis, 0, 0, tiled=False), axis=0)  28.6 us
    reduce_max x2, other arithmetic, col_peaks(): col_local = jnp.max(magnitude * row_pieces[:, :, None], axis=1)  15.7 us
    ppermute x3, starting transfers between devices, butterfly(): value = combine(value, lax.ppermute(value, axis, pairs))  11.6 us
    reduce_sum x2, other arithmetic, forward_local(): forward_products = jnp.sum(matrix * forward_pieces[:, None, :], axis=2)  11.2 us
    ppermute x3, waiting for transfers between devices, butterfly(): value = combine(value, lax.ppermute(value, axis, pairs))  11.1 us
    ppermute x2, waiting for transfers between devices, local(): lax.ppermute(jnp.concatenate([segments, link_sum], axis=0), 'col', [(i, i...  8.62 us
    ppermute x3, waiting for transfers between devices, local(): lax.ppermute(carried, 'col', [(i, i ^ bit) for i in range(n_col)])  7.49 us
  transfers between devices with their start and end apart: 13, of which 13 were waited for; matrix products, arithmetic and copies ran while one was open for 1% of the time, Pallas kernels for 0%

profile of v5, /device:TPU:8, one launch (start us, length us, event | category | flops | bytes accessed | tf_op | source)
XLA Modules:
  0.0 179.1 jit_solution(962503495032152714)
XLA Ops:
  2.8 1.6 gather_fusion.3
  5.8 10.0 %multiply_reduce_fusion.3 = (f32[128,128]{1,0:T(8,128)S(1)}, f32[128,128]{1,0:T(8,128)S(1)}, f32[128,128]{1,0:T(8,128)S(1)}) fusion(f32[1,1,128,128,128]{4,3,2,1,0:T(8,128)} %param.14, f32[128,128]{1,0:T(8,128)S(1)} %get-tuple-element.29, f32[128]{0:T(128)S(1)} %compare_convert_fusion, f32[128,128]{1,0:T(8,128)S(1)} %get-tuple-element.32, ...), kind=kLoop, calls=%fused_computation.25 | loop fusion | flops 16728064 | bytes 8782336 | tf_op jit(solution)/shard_map/reduce_max | solution.py:82
  17.6 7.5 %all-to-all-start = ((f32[32,16,128]{2,1,0:T(8,128)}), f32[32,16,128]{2,1,0:T(8,128)S(1)}, u32[]{:S(2)}, u32[]{:S(2)}) async-start(f32[32,16,128]{2,1,0:T(8,128)} %broadcast_in_dim.106), calls=%async_computation | async-start | bytes 524288 | tf_op jit(solution)/shard_map/all_to_all | solution.py:26
  26.4 6.1 %all-to-all-done = f32[32,16,128]{2,1,0:T(8,128)S(1)} async-done(((f32[32,16,128]{2,1,0:T(8,128)}), f32[32,16,128]{2,1,0:T(8,128)S(1)}, u32[]{:S(2)}, u32[]{:S(2)}) %all-to-all-start) | async-done | bytes 262176 | tf_op jit(solution)/shard_map/all_to_all | solution.py:26
  33.3 5.7 %multiply_reduce_fusion.1 = f32[128,128]{1,0:T(8,128)S(1)} fusion(f32[1,1,128,128,128]{4,3,2,1,0:T(8,128)} %param.14, f32[128,128]{1,0:T(8,128)S(1)} %broadcast_select_fusion.5, f32[128]{0:T(128)S(1)} %compare_convert_fusion), kind=kLoop, calls=%fused_computation.23 | loop fusion | flops 8372224 | bytes 8520192 | tf_op jit(solution)/shard_map/reduce_max | solution.py:82
  40.1 2.0 %collective-permute-start = (f32[192,128]{1,0:T(8,128)S(1)}, f32[192,128]{1,0:T(8,128)S(1)}, u32[]{:S(2)}, u32[]{:S(2)}) collective-permute-start(f32[192,128]{1,0:T(8,128)S(1)} %pad_maximum_fusion), channel_id=1, source_target_pairs={{0,32},{32,0},{64,96},{96,64},{128,160},{160,128},{192,224},{224,1... | collective-permute-start | bytes 294920 | tf_op jit(solution)/shard_map/ppermute | solution.py:19
  42.1 3.5 %collective-permute-done = f32[192,128]{1,0:T(8,128)S(1)} collective-permute-done((f32[192,128]{1,0:T(8,128)S(1)}, f32[192,128]{1,0:T(8,128)S(1)}, u32[]{:S(2)}, u32[]{:S(2)}) %collective-permute-start) | collective-permute-done | bytes 98336 | tf_op jit(solution)/shard_map/ppermute | solution.py:19
  45.7 3.4 %collective-permute-start.1 = (f32[192,128]{1,0:T(8,128)S(1)}, f32[192,128]{1,0:T(8,128)S(1)}, u32[]{:S(2)}, u32[]{:S(2)}) collective-permute-start(f32[192,128]{1,0:T(8,128)S(1)} %pad_maximum_fusion.1), channel_id=1, source_target_pairs={{0,64},{32,96},{64,0},{96,32},{128,192},{160,224},{192,128},{224,1... | collective-permute-start | bytes 294920 | tf_op jit(solution)/shard_map/ppermute | solution.py:19
  49.0 5.0 %collective-permute-done.1 = f32[192,128]{1,0:T(8,128)S(1)} collective-permute-done((f32[192,128]{1,0:T(8,128)S(1)}, f32[192,128]{1,0:T(8,128)S(1)}, u32[]{:S(2)}, u32[]{:S(2)}) %collective-permute-start.1) | collective-permute-done | bytes 98336 | tf_op jit(solution)/shard_map/ppermute | solution.py:19
  54.0 6.3 %collective-permute-start.2 = (f32[192,128]{1,0:T(8,128)S(1)}, f32[192,128]{1,0:T(8,128)S(1)}, u32[]{:S(2)}, u32[]{:S(2)}) collective-permute-start(f32[192,128]{1,0:T(8,128)S(1)} %pad_maximum_fusion.2), channel_id=1, source_target_pairs={{0,128},{32,160},{64,192},{96,224},{128,0},{160,32},{192,64},{224,... | collective-permute-start | bytes 294920 | tf_op jit(solution)/shard_map/ppermute | solution.py:19
  60.3 2.6 %collective-permute-done.2 = f32[192,128]{1,0:T(8,128)S(1)} collective-permute-done((f32[192,128]{1,0:T(8,128)S(1)}, f32[192,128]{1,0:T(8,128)S(1)}, u32[]{:S(2)}, u32[]{:S(2)}) %collective-permute-start.2) | collective-permute-done | bytes 98336 | tf_op jit(solution)/shard_map/ppermute | solution.py:19
  64.3 5.8 %multiply_reduce_fusion = f32[128,128]{1,0:T(8,128)S(1)} fusion(f32[1,1,128,128,128]{4,3,2,1,0:T(8,128)} %param.14, f32[128,128]{1,0:T(8,128)S(1)} %broadcast_select_fusion.3, f32[128]{0:T(128)S(1)} %compare_convert_fusion), kind=kLoop, calls=%fused_computation.22 | loop fusion | flops 8372224 | bytes 8520192 | tf_op jit(solution)/shard_map/reduce_max | solution.py:77
  71.9 1.3 and_select_fusion
  73.9 4.8 %all-to-all-start.1 = ((f32[32,17,128]{2,1,0:T(8,128)}), f32[32,17,128]{2,1,0:T(8,128)S(1)}, u32[]{:S(2)}, u32[]{:S(2)}) async-start(f32[32,17,128]{2,1,0:T(8,128)} %broadcast_in_dim.111), calls=%async_computation.1 | async-start | bytes 786432 | tf_op jit(solution)/shard_map/all_to_all | solution.py:26
  79.4 7.9 %all-to-all-done.1 = f32[32,17,128]{2,1,0:T(8,128)S(1)} async-done(((f32[32,17,128]{2,1,0:T(8,128)}), f32[32,17,128]{2,1,0:T(8,128)S(1)}, u32[]{:S(2)}, u32[]{:S(2)}) %all-to-all-start.1) | async-done | bytes 278560 | tf_op jit(solution)/shard_map/all_to_all | solution.py:26
  90.7 7.4 %all-to-all-start.2 = ((f32[8,1,128]{2,1,0:T(1,128)}), f32[8,1,128]{2,1,0:T(1,128)S(1)}, u32[]{:S(2)}, u32[]{:S(2)}) async-start(f32[8,1,128]{2,1,0:T(1,128)} %broadcast_in_dim.114), calls=%async_computation.2 | async-start | bytes 8192 | tf_op jit(solution)/shard_map/all_to_all | solution.py:26
  99.6 6.2 %all-to-all-done.2 = f32[8,1,128]{2,1,0:T(1,128)S(1)} async-done(((f32[8,1,128]{2,1,0:T(1,128)}), f32[8,1,128]{2,1,0:T(1,128)S(1)}, u32[]{:S(2)}, u32[]{:S(2)}) %all-to-all-start.2) | async-done | bytes 4128 | tf_op jit(solution)/shard_map/all_to_all | solution.py:26
  106.7 5.6 %fusion.4 = f32[128,128]{1,0:T(8,128)S(1)} fusion(f32[1,1,128,128,128]{4,3,2,1,0:T(8,128)} %param.14, f32[128,128]{1,0:T(8,128)S(1)} %broadcast_select_fusion.2), kind=kLoop, calls=%fused_computation.20 | loop fusion | flops 4177920 | bytes 8519680 | tf_op jit(solution)/shard_map/reduce_sum | solution.py:144
  113.4 5.4 %all-to-all-start.3 = ((f32[32,16,128]{2,1,0:T(8,128)}), f32[32,16,128]{2,1,0:T(8,128)S(1)}, u32[]{:S(2)}, u32[]{:S(2)}) async-start(f32[32,16,128]{2,1,0:T(8,128)} %broadcast_in_dim.115), calls=%async_computation.3 | async-start | bytes 524288 | tf_op jit(solution)/shard_map/all_to_all | solution.py:26
  118.8 7.4 %all-to-all-done.3 = f32[32,16,128]{2,1,0:T(8,128)S(1)} async-done(((f32[32,16,128]{2,1,0:T(8,128)}), f32[32,16,128]{2,1,0:T(8,128)S(1)}, u32[]{:S(2)}, u32[]{:S(2)}) %all-to-all-start.3) | async-done | bytes 262176 | tf_op jit(solution)/shard_map/all_to_all | solution.py:26
  127.0 5.7 %fusion = f32[128,1,128]{2,1,0:T(1,128)S(1)} fusion(f32[128,128,1]{1,2,0:T(1,128)S(1)} %bitcast.113, f32[1,1,128,128,128]{4,3,2,1,0:T(8,128)} %param.14), kind=kOutput, calls=%fused_computation.13 | convolution fusion | flops 12582912 | bytes 8519680 | tf_op jit(solution)/shard_map/tij,ti->tj/dot_general | solution.py:139
  133.6 3.4 %all-to-all-start.4 = ((f32[8,64,128]{2,1,0:T(8,128)}), f32[8,64,128]{2,1,0:T(8,128)S(1)}, u32[]{:S(2)}, u32[]{:S(2)}) async-start(f32[8,64,128]{2,1,0:T(8,128)} %broadcast_in_dim.116), calls=%async_computation.4 | async-start | bytes 524288 | tf_op jit(solution)/shard_map/all_to_all | solution.py:26
  137.1 12.7 %all-to-all-done.4 = f32[8,64,128]{2,1,0:T(8,128)S(1)} async-done(((f32[8,64,128]{2,1,0:T(8,128)}), f32[8,64,128]{2,1,0:T(8,128)S(1)}, u32[]{:S(2)}, u32[]{:S(2)}) %all-to-all-start.4) | async-done | bytes 262176 | tf_op jit(solution)/shard_map/all_to_all | solution.py:26
  151.2 5.6 %fusion.5 = f32[128,128]{1,0:T(8,128)S(1)} fusion(f32[1,1,128,128,128]{4,3,2,1,0:T(8,128)} %param.14, f32[128,128]{1,0:T(8,128)S(1)} %broadcast_select_fusion), kind=kLoop, calls=%fused_computation.21 | loop fusion | flops 4177920 | bytes 8519680 | tf_op jit(solution)/shard_map/reduce_sum | solution.py:144
  157.3 1.1 collective-permute-done.3
  158.5 1.5 collective-permute-start.4
  160.0 2.5 %collective-permute-done.4 = f32[80,128]{1,0:T(8,128)S(1)} collective-permute-done((f32[80,128]{1,0:T(8,128)S(1)}, f32[80,128]{1,0:T(8,128)S(1)}, u32[]{:S(2)}, u32[]{:S(2)}) %collective-permute-start.4) | collective-permute-done | bytes 40992 | tf_op jit(solution)/shard_map/ppermute | solution.py:171
  162.5 1.6 collective-permute-start.5
  164.1 3.9 %collective-permute-done.5 = f32[80,128]{1,0:T(8,128)S(1)} collective-permute-done((f32[80,128]{1,0:T(8,128)S(1)}, f32[80,128]{1,0:T(8,128)S(1)}, u32[]{:S(2)}, u32[]{:S(2)}) %collective-permute-start.5) | collective-permute-done | bytes 40992 | tf_op jit(solution)/shard_map/ppermute | solution.py:171
  168.7 3.7 %collective-permute-done.6 = f32[80,128]{1,0:T(8,128)S(1)} collective-permute-done((f32[80,128]{1,0:T(8,128)S(1)}, f32[80,128]{1,0:T(8,128)S(1)}, u32[]{:S(2)}, u32[]{:S(2)}) %collective-permute-start.6) | collective-permute-done | bytes 40992 | tf_op jit(solution)/shard_map/ppermute | solution.py:178
  172.5 1.1 collective-permute-start.7
  173.5 4.9 %collective-permute-done.7 = f32[144,128]{1,0:T(8,128)S(1)} collective-permute-done((f32[144,128]{1,0:T(8,128)S(1)}, f32[144,128]{1,0:T(8,128)S(1)}, u32[]{:S(2)}, u32[]{:S(2)}) %collective-permute-start.7) | collective-permute-done | bytes 73760 | tf_op jit(solution)/shard_map/ppermute | solution.py:178
  (96 shorter events, 21.3 us)
Async XLA Ops:
  15.8 47.1 %copy-start.2 = (f32[8192]{0:T(1024)S(1)}, f32[8192]{0:T(1024)}, u32[]{:S(2)}) copy-start(f32[8192]{0:T(1024)} %param.17) | copy-start | bytes 98308
  17.6 14.9 %all-to-all-start = ((f32[32,16,128]{2,1,0:T(8,128)}), f32[32,16,128]{2,1,0:T(8,128)S(1)}, u32[]{:S(2)}, u32[]{:S(2)}) async-start(f32[32,16,128]{2,1,0:T(8,128)} %broadcast_in_dim.106), calls=%async_computation | async-start | bytes 524288 | tf_op jit(solution)/shard_map/all_to_all | solution.py:26
  33.3 37.8 %copy-start.1 = (f32[34816]{0:T(1024)S(1)}, f32[34816]{0:T(1024)}, u32[]{:S(2)}) copy-start(f32[34816]{0:T(1024)} %param.20) | copy-start | bytes 417796
  39.0 66.9 %copy-start.3 = (f32[8192]{0:T(1024)S(1)}, f32[8192]{0:T(1024)}, u32[]{:S(2)}) copy-start(f32[8192]{0:T(1024)} %param.18) | copy-start | bytes 98308
  39.0 66.9 %copy-start.4 = (f32[8192]{0:T(1024)S(1)}, f32[8192]{0:T(1024)}, u32[]{:S(2)}) copy-start(f32[8192]{0:T(1024)} %param.19) | copy-start | bytes 98308
  39.1 66.9 %copy-start.5 = (f32[8192]{0:T(1024)S(1)}, f32[8192]{0:T(1024)}, u32[]{:S(2)}) copy-start(f32[8192]{0:T(1024)} %param.21) | copy-start | bytes 98308
  40.1 5.5 %collective-permute-start = (f32[192,128]{1,0:T(8,128)S(1)}, f32[192,128]{1,0:T(8,128)S(1)}, u32[]{:S(2)}, u32[]{:S(2)}) collective-permute-start(f32[192,128]{1,0:T(8,128)S(1)} %pad_maximum_fusion), channel_id=1, source_target_pairs={{0,32},{32,0},{64,96},{96,64},{128,160},{160,128},{192,224},{224,1... | collective-permute-start | bytes 294920 | tf_op jit(solution)/shard_map/ppermute | solution.py:19
  45.7 8.3 %collective-permute-start.1 = (f32[192,128]{1,0:T(8,128)S(1)}, f32[192,128]{1,0:T(8,128)S(1)}, u32[]{:S(2)}, u32[]{:S(2)}) collective-permute-start(f32[192,128]{1,0:T(8,128)S(1)} %pad_maximum_fusion.1), channel_id=1, source_target_pairs={{0,64},{32,96},{64,0},{96,32},{128,192},{160,224},{192,128},{224,1... | collective-permute-start | bytes 294920 | tf_op jit(solution)/shard_map/ppermute | solution.py:19
  54.0 8.9 %collective-permute-start.2 = (f32[192,128]{1,0:T(8,128)S(1)}, f32[192,128]{1,0:T(8,128)S(1)}, u32[]{:S(2)}, u32[]{:S(2)}) collective-permute-start(f32[192,128]{1,0:T(8,128)S(1)} %pad_maximum_fusion.2), channel_id=1, source_target_pairs={{0,128},{32,160},{64,192},{96,224},{128,0},{160,32},{192,64},{224,... | collective-permute-start | bytes 294920 | tf_op jit(solution)/shard_map/ppermute | solution.py:19
  70.1 56.1 %copy-start = (f32[34816]{0:T(1024)S(1)}, f32[34816]{0:T(1024)}, u32[]{:S(2)}) copy-start(f32[34816]{0:T(1024)} %param.22) | copy-start | bytes 417796
  73.9 13.4 %all-to-all-start.1 = ((f32[32,17,128]{2,1,0:T(8,128)}), f32[32,17,128]{2,1,0:T(8,128)S(1)}, u32[]{:S(2)}, u32[]{:S(2)}) async-start(f32[32,17,128]{2,1,0:T(8,128)} %broadcast_in_dim.111), calls=%async_computation.1 | async-start | bytes 786432 | tf_op jit(solution)/shard_map/all_to_all | solution.py:26
  90.7 15.1 %all-to-all-start.2 = ((f32[8,1,128]{2,1,0:T(1,128)}), f32[8,1,128]{2,1,0:T(1,128)S(1)}, u32[]{:S(2)}, u32[]{:S(2)}) async-start(f32[8,1,128]{2,1,0:T(1,128)} %broadcast_in_dim.114), calls=%async_computation.2 | async-start | bytes 8192 | tf_op jit(solution)/shard_map/all_to_all | solution.py:26
  113.4 12.8 %all-to-all-start.3 = ((f32[32,16,128]{2,1,0:T(8,128)}), f32[32,16,128]{2,1,0:T(8,128)S(1)}, u32[]{:S(2)}, u32[]{:S(2)}) async-start(f32[32,16,128]{2,1,0:T(8,128)} %broadcast_in_dim.115), calls=%async_computation.3 | async-start | bytes 524288 | tf_op jit(solution)/shard_map/all_to_all | solution.py:26
  133.6 16.2 %all-to-all-start.4 = ((f32[8,64,128]{2,1,0:T(8,128)}), f32[8,64,128]{2,1,0:T(8,128)S(1)}, u32[]{:S(2)}, u32[]{:S(2)}) async-start(f32[8,64,128]{2,1,0:T(8,128)} %broadcast_in_dim.116), calls=%async_computation.4 | async-start | bytes 524288 | tf_op jit(solution)/shard_map/all_to_all | solution.py:26
  157.2 1.3 collective-permute-start.3
  158.5 4.0 %collective-permute-start.4 = (f32[80,128]{1,0:T(8,128)S(1)}, f32[80,128]{1,0:T(8,128)S(1)}, u32[]{:S(2)}, u32[]{:S(2)}) collective-permute-start(f32[80,128]{1,0:T(8,128)S(1)} %fusion.72), channel_id=1, source_target_pairs={{0,2},{1,3},{2,0},{3,1},{4,6},{5,7},{6,4},{7,5},{8,10},{9,11},{10,... | collective-permute-start | bytes 122888 | tf_op jit(solution)/shard_map/ppermute | solution.py:171
  162.5 5.5 %collective-permute-start.5 = (f32[80,128]{1,0:T(8,128)S(1)}, f32[80,128]{1,0:T(8,128)S(1)}, u32[]{:S(2)}, u32[]{:S(2)}) collective-permute-start(f32[80,128]{1,0:T(8,128)S(1)} %add.111), channel_id=1, source_target_pairs={{0,4},{1,5},{2,6},{3,7},{4,0},{5,1},{6,2},{7,3},{8,12},{9,13},{10,... | collective-permute-start | bytes 122888 | tf_op jit(solution)/shard_map/ppermute | solution.py:171
  168.0 4.4 %collective-permute-start.6 = (f32[80,128]{1,0:T(8,128)S(1)}, f32[80,128]{1,0:T(8,128)S(1)}, u32[]{:S(2)}, u32[]{:S(2)}) collective-permute-start(f32[80,128]{1,0:T(8,128)S(1)} %add.112), channel_id=1, source_target_pairs={{0,8},{1,9},{2,10},{3,11},{4,12},{5,13},{6,14},{7,15},{8,0},{9,1},... | collective-permute-start | bytes 122888 | tf_op jit(solution)/shard_map/ppermute | solution.py:178
  172.5 5.9 %collective-permute-start.7 = (f32[144,128]{1,0:T(8,128)S(1)}, f32[144,128]{1,0:T(8,128)S(1)}, u32[]{:S(2)}, u32[]{:S(2)}) collective-permute-start(f32[144,128]{1,0:T(8,128)S(1)} %pad_maximum_fusion.3), channel_id=1, source_target_pairs={{0,16},{1,17},{2,18},{3,19},{4,20},{5,21},{6,22},{7,23},{8,24},{9,... | collective-permute-start | bytes 221192 | tf_op jit(solution)/shard_map/ppermute | solution.py:178

commit v6 on v5

--- a/solution.py
+++ b/solution.py
@@ -166,26 +166,11 @@
                 own_out = jnp.where(own_period, row_scale * own_dual, 0.0)
                 segment = lax.dynamic_slice_in_dim(own_out, seg_start, col_blocks, axis=0)
                 carried = jnp.concatenate([segment, partial_rows[link_start:]], axis=0)
-                bit = 1
-                while bit < n_row:
-                    carried = carried + lax.ppermute(carried, "col", [(i, i ^ bit) for i in range(n_col)])
-                    bit *= 2
-                segments = carried[:col_blocks]
-                link_sum = carried[col_blocks:]
-                group = c // n_row
-                while bit < n_col:
-                    held = segments.shape[0]
-                    other = lax.ppermute(
-                        jnp.concatenate([segments, link_sum], axis=0), "col", [(i, i ^ bit) for i in range(n_col)]
-                    )
-                    upper_half = (group & (bit // n_row)) != 0
-                    segments = jnp.where(
-                        upper_half,
-                        jnp.concatenate([other[:held], segments], axis=0),
-                        jnp.concatenate([segments, other[:held]], axis=0),
-                    )
-                    link_sum = link_sum + other[held:]
-                    bit *= 2
+                spread = jnp.broadcast_to(carried[None], (n_col,) + carried.shape)
+                received = lax.all_to_all(spread, "col", 0, 0, tiled=False)
+                link_sum = jnp.sum(received[:, col_blocks:], axis=0)
+                owners = r + n_row * jnp.arange(n_col // n_row, dtype=jnp.int32)
+                segments = jnp.take(received[:, :col_blocks], owners, axis=0).reshape(link_start, tile_width)
                 joined = jnp.concatenate([segments, link_sum], axis=0)
                 link_dual = jnp.maximum(
                     dual[link_start:]

time: 180 us -> 187 us (1.039); the launches traced: 179 us -> 183 us
  waiting for transfers between devices: 67.5 us -> 69.5 us
  local copies, waits for them, and re-layouts: 9.74 us -> 11.7 us
    all_to_all x0 -> x1, waiting for transfers between devices: none -> 18.1 us  [local(): received = lax.all_to_all(spread, 'col', 0, 0, tiled=False)]
    ppermute x5 -> x0, waiting for transfers between devices: 16.1 us -> none  [the longest x2 8.62 us: local(): lax.ppermute(jnp.concatenate([segments, link_sum], axis=0), 'col', [(i, i...]
    all_to_all x0 -> x1, starting transfers between devices: none -> 5.14 us  [local(): received = lax.all_to_all(spread, 'col', 0, 0, tiled=False)]
    ppermute x5 -> x0, starting transfers between devices: 5.08 us -> none  [the longest x3 3.32 us: local(): lax.ppermute(carried, 'col', [(i, i ^ bit) for i in range(n_col)])]
  transfers between devices with their start and end apart: 13 -> 9, of which waited for: 13 -> 9; matrix products, arithmetic and copies ran while one was open for 1% -> 1% of each run, Pallas kernels for 0% -> 0%
where the time goes in v6:
time: 187 us; the launch traced here: 183 us
  waiting for transfers between devices  69.5 us (37%)
  other arithmetic  45.5 us (24%)
  starting transfers between devices  45.4 us (24%)
  local copies, waits for them, and re-layouts  11.7 us (6%)
  matrix products  6.57 us (4%)
  between operations  4.67 us (2%)
    all_to_all x5, waiting for transfers between devices, exchange(): return reduce(lax.all_to_all(spread, axis, 0, 0, tiled=False), axis=0)  40.3 us
    all_to_all x5, starting transfers between devices, exchange(): return reduce(lax.all_to_all(spread, axis, 0, 0, tiled=False), axis=0)  28.6 us
    all_to_all x1, waiting for transfers between devices, local(): received = lax.all_to_all(spread, 'col', 0, 0, tiled=False)  18.1 us
    reduce_max x2, other arithmetic, col_peaks(): col_local = jnp.max(magnitude * row_pieces[:, :, None], axis=1)  15.7 us
    ppermute x3, starting transfers between devices, butterfly(): value = combine(value, lax.ppermute(value, axis, pairs))  11.6 us
    reduce_sum x2, other arithmetic, forward_local(): forward_products = jnp.sum(matrix * forward_pieces[:, None, :], axis=2)  11.2 us
    ppermute x3, waiting for transfers between devices, butterfly(): value = combine(value, lax.ppermute(value, axis, pairs))  11.1 us
    reduce_max x1, other arithmetic, row_peaks(): row_local = jnp.max(magnitude * col_pieces[:, None, :], axis=2)  5.77 us
  transfers between devices with their start and end apart: 9, of which 9 were waited for; matrix products, arithmetic and copies ran while one was open for 1% of the time, Pallas kernels for 0%

profile of v6, /device:TPU:8, one launch (start us, length us, event | category | flops | bytes accessed | tf_op | source)
XLA Modules:
  0.0 183.3 jit_solution(2244453368439398019)
XLA Ops:
  0.6 0.8 compare_and_fusion
  2.2 1.6 gather_fusion.4
  5.8 10.0 %multiply_reduce_fusion.3 = (f32[128,128]{1,0:T(8,128)S(1)}, f32[128,128]{1,0:T(8,128)S(1)}, f32[128,128]{1,0:T(8,128)S(1)}) fusion(f32[1,1,128,128,128]{4,3,2,1,0:T(8,128)} %param.14, f32[128,128]{1,0:T(8,128)S(1)} %get-tuple-element.29, f32[128]{0:T(128)S(1)} %compare_convert_fusion, f32[128,128]{1,0:T(8,128)S(1)} %get-tuple-element.32, ...), kind=kLoop, calls=%fused_computation.26 | loop fusion | flops 16728064 | bytes 8782336 | tf_op jit(solution)/shard_map/reduce_max | solution.py:82
  15.8 1.0 scatter_custom_fusion.1
  17.6 7.5 %all-to-all-start = ((f32[32,16,128]{2,1,0:T(8,128)}), f32[32,16,128]{2,1,0:T(8,128)S(1)}, u32[]{:S(2)}, u32[]{:S(2)}) async-start(f32[32,16,128]{2,1,0:T(8,128)} %broadcast_in_dim.126), calls=%async_computation | async-start | bytes 524288 | tf_op jit(solution)/shard_map/all_to_all | solution.py:26
  25.1 1.0 scatter_custom_fusion
  26.4 6.1 %all-to-all-done = f32[32,16,128]{2,1,0:T(8,128)S(1)} async-done(((f32[32,16,128]{2,1,0:T(8,128)}), f32[32,16,128]{2,1,0:T(8,128)S(1)}, u32[]{:S(2)}, u32[]{:S(2)}) %all-to-all-start) | async-done | bytes 262176 | tf_op jit(solution)/shard_map/all_to_all | solution.py:26
  33.3 5.7 %multiply_reduce_fusion.1 = f32[128,128]{1,0:T(8,128)S(1)} fusion(f32[1,1,128,128,128]{4,3,2,1,0:T(8,128)} %param.14, f32[128,128]{1,0:T(8,128)S(1)} %broadcast_select_fusion.5, f32[128]{0:T(128)S(1)} %compare_convert_fusion), kind=kLoop, calls=%fused_computation.24 | loop fusion | flops 8372224 | bytes 8520192 | tf_op jit(solution)/shard_map/reduce_max | solution.py:82
  39.1 1.0 scatter_custom_fusion.2
  40.1 2.0 %collective-permute-start = (f32[192,128]{1,0:T(8,128)S(1)}, f32[192,128]{1,0:T(8,128)S(1)}, u32[]{:S(2)}, u32[]{:S(2)}) collective-permute-start(f32[192,128]{1,0:T(8,128)S(1)} %pad_maximum_fusion), channel_id=1, source_target_pairs={{0,32},{32,0},{64,96},{96,64},{128,160},{160,128},{192,224},{224,1... | collective-permute-start | bytes 294920 | tf_op jit(solution)/shard_map/ppermute | solution.py:19
  42.1 3.5 %collective-permute-done = f32[192,128]{1,0:T(8,128)S(1)} collective-permute-done((f32[192,128]{1,0:T(8,128)S(1)}, f32[192,128]{1,0:T(8,128)S(1)}, u32[]{:S(2)}, u32[]{:S(2)}) %collective-permute-start) | collective-permute-done | bytes 98336 | tf_op jit(solution)/shard_map/ppermute | solution.py:19
  45.7 3.4 %collective-permute-start.1 = (f32[192,128]{1,0:T(8,128)S(1)}, f32[192,128]{1,0:T(8,128)S(1)}, u32[]{:S(2)}, u32[]{:S(2)}) collective-permute-start(f32[192,128]{1,0:T(8,128)S(1)} %pad_maximum_fusion.1), channel_id=1, source_target_pairs={{0,64},{32,96},{64,0},{96,32},{128,192},{160,224},{192,128},{224,1... | collective-permute-start | bytes 294920 | tf_op jit(solution)/shard_map/ppermute | solution.py:19
  49.0 5.0 %collective-permute-done.1 = f32[192,128]{1,0:T(8,128)S(1)} collective-permute-done((f32[192,128]{1,0:T(8,128)S(1)}, f32[192,128]{1,0:T(8,128)S(1)}, u32[]{:S(2)}, u32[]{:S(2)}) %collective-permute-start.1) | collective-permute-done | bytes 98336 | tf_op jit(solution)/shard_map/ppermute | solution.py:19
  54.0 6.3 %collective-permute-start.2 = (f32[192,128]{1,0:T(8,128)S(1)}, f32[192,128]{1,0:T(8,128)S(1)}, u32[]{:S(2)}, u32[]{:S(2)}) collective-permute-start(f32[192,128]{1,0:T(8,128)S(1)} %pad_maximum_fusion.2), channel_id=1, source_target_pairs={{0,128},{32,160},{64,192},{96,224},{128,0},{160,32},{192,64},{224,... | collective-permute-start | bytes 294920 | tf_op jit(solution)/shard_map/ppermute | solution.py:19
  60.3 2.6 %collective-permute-done.2 = f32[192,128]{1,0:T(8,128)S(1)} collective-permute-done((f32[192,128]{1,0:T(8,128)S(1)}, f32[192,128]{1,0:T(8,128)S(1)}, u32[]{:S(2)}, u32[]{:S(2)}) %collective-permute-start.2) | collective-permute-done | bytes 98336 | tf_op jit(solution)/shard_map/ppermute | solution.py:19
  64.3 5.8 %multiply_reduce_fusion = f32[128,128]{1,0:T(8,128)S(1)} fusion(f32[1,1,128,128,128]{4,3,2,1,0:T(8,128)} %param.14, f32[128,128]{1,0:T(8,128)S(1)} %broadcast_select_fusion.3, f32[128]{0:T(128)S(1)} %compare_convert_fusion), kind=kLoop, calls=%fused_computation.23 | loop fusion | flops 8372224 | bytes 8520192 | tf_op jit(solution)/shard_map/reduce_max | solution.py:77
  70.1 1.0 scatter_custom_fusion.3
  71.9 1.3 and_select_fusion
  74.0 4.8 %all-to-all-start.1 = ((f32[32,17,128]{2,1,0:T(8,128)}), f32[32,17,128]{2,1,0:T(8,128)S(1)}, u32[]{:S(2)}, u32[]{:S(2)}) async-start(f32[32,17,128]{2,1,0:T(8,128)} %broadcast_in_dim.131), calls=%async_computation.1 | async-start | bytes 786432 | tf_op jit(solution)/shard_map/all_to_all | solution.py:26
  79.5 7.9 %all-to-all-done.1 = f32[32,17,128]{2,1,0:T(8,128)S(1)} async-done(((f32[32,17,128]{2,1,0:T(8,128)}), f32[32,17,128]{2,1,0:T(8,128)S(1)}, u32[]{:S(2)}, u32[]{:S(2)}) %all-to-all-start.1) | async-done | bytes 278560 | tf_op jit(solution)/shard_map/all_to_all | solution.py:26
  90.7 7.4 %all-to-all-start.2 = ((f32[8,1,128]{2,1,0:T(1,128)}), f32[8,1,128]{2,1,0:T(1,128)S(1)}, u32[]{:S(2)}, u32[]{:S(2)}) async-start(f32[8,1,128]{2,1,0:T(1,128)} %broadcast_in_dim.134), calls=%async_computation.2 | async-start | bytes 8192 | tf_op jit(solution)/shard_map/all_to_all | solution.py:26
  99.6 6.2 %all-to-all-done.2 = f32[8,1,128]{2,1,0:T(1,128)S(1)} async-done(((f32[8,1,128]{2,1,0:T(1,128)}), f32[8,1,128]{2,1,0:T(1,128)S(1)}, u32[]{:S(2)}, u32[]{:S(2)}) %all-to-all-start.2) | async-done | bytes 4128 | tf_op jit(solution)/shard_map/all_to_all | solution.py:26
  106.8 5.6 %fusion.4 = f32[128,128]{1,0:T(8,128)S(1)} fusion(f32[1,1,128,128,128]{4,3,2,1,0:T(8,128)} %param.14, f32[128,128]{1,0:T(8,128)S(1)} %broadcast_select_fusion.2), kind=kLoop, calls=%fused_computation.21 | loop fusion | flops 4177920 | bytes 8519680 | tf_op jit(solution)/shard_map/reduce_sum | solution.py:144
  113.4 5.4 %all-to-all-start.3 = ((f32[32,16,128]{2,1,0:T(8,128)}), f32[32,16,128]{2,1,0:T(8,128)S(1)}, u32[]{:S(2)}, u32[]{:S(2)}) async-start(f32[32,16,128]{2,1,0:T(8,128)} %broadcast_in_dim.135), calls=%async_computation.3 | async-start | bytes 524288 | tf_op jit(solution)/shard_map/all_to_all | solution.py:26
  118.8 7.4 %all-to-all-done.3 = f32[32,16,128]{2,1,0:T(8,128)S(1)} async-done(((f32[32,16,128]{2,1,0:T(8,128)}), f32[32,16,128]{2,1,0:T(8,128)S(1)}, u32[]{:S(2)}, u32[]{:S(2)}) %all-to-all-start.3) | async-done | bytes 262176 | tf_op jit(solution)/shard_map/all_to_all | solution.py:26
  127.0 5.7 %fusion = f32[128,1,128]{2,1,0:T(1,128)S(1)} fusion(f32[128,128,1]{1,2,0:T(1,128)S(1)} %bitcast.117, f32[1,1,128,128,128]{4,3,2,1,0:T(8,128)} %param.14), kind=kOutput, calls=%fused_computation.14 | convolution fusion | flops 12582912 | bytes 8519680 | tf_op jit(solution)/shard_map/tij,ti->tj/dot_general | solution.py:139
  133.6 3.4 %all-to-all-start.4 = ((f32[8,64,128]{2,1,0:T(8,128)}), f32[8,64,128]{2,1,0:T(8,128)S(1)}, u32[]{:S(2)}, u32[]{:S(2)}) async-start(f32[8,64,128]{2,1,0:T(8,128)} %broadcast_in_dim.136), calls=%async_computation.4 | async-start | bytes 524288 | tf_op jit(solution)/shard_map/all_to_all | solution.py:26
  137.1 12.7 %all-to-all-done.4 = f32[8,64,128]{2,1,0:T(8,128)S(1)} async-done(((f32[8,64,128]{2,1,0:T(8,128)}), f32[8,64,128]{2,1,0:T(8,128)S(1)}, u32[]{:S(2)}, u32[]{:S(2)}) %all-to-all-start.4) | async-done | bytes 262176 | tf_op jit(solution)/shard_map/all_to_all | solution.py:26
  151.2 5.6 %fusion.5 = f32[128,128]{1,0:T(8,128)S(1)} fusion(f32[1,1,128,128,128]{4,3,2,1,0:T(8,128)} %param.14, f32[128,128]{1,0:T(8,128)S(1)} %broadcast_select_fusion), kind=kLoop, calls=%fused_computation.22 | loop fusion | flops 4177920 | bytes 8519680 | tf_op jit(solution)/shard_map/reduce_sum | solution.py:144
  157.2 1.1 broadcast_in_dim.140
  158.3 5.1 %all-to-all-start.5 = ((f32[32,80,128]{2,1,0:T(8,128)}), f32[32,80,128]{2,1,0:T(8,128)S(1)}, u32[]{:S(2)}, u32[]{:S(2)}) async-start(f32[32,80,128]{2,1,0:T(8,128)} %broadcast_in_dim.140), calls=%async_computation.5 | async-start | bytes 2621440 | tf_op jit(solution)/shard_map/all_to_all | solution.py:170
  163.7 18.1 %all-to-all-done.5 = f32[32,80,128]{2,1,0:T(8,128)S(1)} async-done(((f32[32,80,128]{2,1,0:T(8,128)}), f32[32,80,128]{2,1,0:T(8,128)S(1)}, u32[]{:S(2)}, u32[]{:S(2)}) %all-to-all-start.5) | async-done | bytes 1310752 | tf_op jit(solution)/shard_map/all_to_all | solution.py:170
  (88 shorter events, 16.5 us)
Async XLA Ops:
  15.8 47.1 %copy-start.2 = (f32[8192]{0:T(1024)S(1)}, f32[8192]{0:T(1024)}, u32[]{:S(2)}) copy-start(f32[8192]{0:T(1024)} %param.17) | copy-start | bytes 98308
  17.6 14.9 %all-to-all-start = ((f32[32,16,128]{2,1,0:T(8,128)}), f32[32,16,128]{2,1,0:T(8,128)S(1)}, u32[]{:S(2)}, u32[]{:S(2)}) async-start(f32[32,16,128]{2,1,0:T(8,128)} %broadcast_in_dim.126), calls=%async_computation | async-start | bytes 524288 | tf_op jit(solution)/shard_map/all_to_all | solution.py:26
  33.3 37.9 %copy-start.1 = (f32[34816]{0:T(1024)S(1)}, f32[34816]{0:T(1024)}, u32[]{:S(2)}) copy-start(f32[34816]{0:T(1024)} %param.20) | copy-start | bytes 417796
  39.0 66.9 %copy-start.3 = (f32[8192]{0:T(1024)S(1)}, f32[8192]{0:T(1024)}, u32[]{:S(2)}) copy-start(f32[8192]{0:T(1024)} %param.18) | copy-start | bytes 98308
  39.0 66.9 %copy-start.4 = (f32[8192]{0:T(1024)S(1)}, f32[8192]{0:T(1024)}, u32[]{:S(2)}) copy-start(f32[8192]{0:T(1024)} %param.19) | copy-start | bytes 98308
  39.1 66.9 %copy-start.5 = (f32[8192]{0:T(1024)S(1)}, f32[8192]{0:T(1024)}, u32[]{:S(2)}) copy-start(f32[8192]{0:T(1024)} %param.21) | copy-start | bytes 98308
  40.1 5.5 %collective-permute-start = (f32[192,128]{1,0:T(8,128)S(1)}, f32[192,128]{1,0:T(8,128)S(1)}, u32[]{:S(2)}, u32[]{:S(2)}) collective-permute-start(f32[192,128]{1,0:T(8,128)S(1)} %pad_maximum_fusion), channel_id=1, source_target_pairs={{0,32},{32,0},{64,96},{96,64},{128,160},{160,128},{192,224},{224,1... | collective-permute-start | bytes 294920 | tf_op jit(solution)/shard_map/ppermute | solution.py:19
  45.7 8.3 %collective-permute-start.1 = (f32[192,128]{1,0:T(8,128)S(1)}, f32[192,128]{1,0:T(8,128)S(1)}, u32[]{:S(2)}, u32[]{:S(2)}) collective-permute-start(f32[192,128]{1,0:T(8,128)S(1)} %pad_maximum_fusion.1), channel_id=1, source_target_pairs={{0,64},{32,96},{64,0},{96,32},{128,192},{160,224},{192,128},{224,1... | collective-permute-start | bytes 294920 | tf_op jit(solution)/shard_map/ppermute | solution.py:19
  54.0 8.9 %collective-permute-start.2 = (f32[192,128]{1,0:T(8,128)S(1)}, f32[192,128]{1,0:T(8,128)S(1)}, u32[]{:S(2)}, u32[]{:S(2)}) collective-permute-start(f32[192,128]{1,0:T(8,128)S(1)} %pad_maximum_fusion.2), channel_id=1, source_target_pairs={{0,128},{32,160},{64,192},{96,224},{128,0},{160,32},{192,64},{224,... | collective-permute-start | bytes 294920 | tf_op jit(solution)/shard_map/ppermute | solution.py:19
  70.1 56.1 %copy-start = (f32[34816]{0:T(1024)S(1)}, f32[34816]{0:T(1024)}, u32[]{:S(2)}) copy-start(f32[34816]{0:T(1024)} %param.22) | copy-start | bytes 417796
  74.0 13.4 %all-to-all-start.1 = ((f32[32,17,128]{2,1,0:T(8,128)}), f32[32,17,128]{2,1,0:T(8,128)S(1)}, u32[]{:S(2)}, u32[]{:S(2)}) async-start(f32[32,17,128]{2,1,0:T(8,128)} %broadcast_in_dim.131), calls=%async_computation.1 | async-start | bytes 786432 | tf_op jit(solution)/shard_map/all_to_all | solution.py:26
  90.7 15.1 %all-to-all-start.2 = ((f32[8,1,128]{2,1,0:T(1,128)}), f32[8,1,128]{2,1,0:T(1,128)S(1)}, u32[]{:S(2)}, u32[]{:S(2)}) async-start(f32[8,1,128]{2,1,0:T(1,128)} %broadcast_in_dim.134), calls=%async_computation.2 | async-start | bytes 8192 | tf_op jit(solution)/shard_map/all_to_all | solution.py:26
  113.4 12.8 %all-to-all-start.3 = ((f32[32,16,128]{2,1,0:T(8,128)}), f32[32,16,128]{2,1,0:T(8,128)S(1)}, u32[]{:S(2)}, u32[]{:S(2)}) async-start(f32[32,16,128]{2,1,0:T(8,128)} %broadcast_in_dim.135), calls=%async_computation.3 | async-start | bytes 524288 | tf_op jit(solution)/shard_map/all_to_all | solution.py:26
  133.6 16.2 %all-to-all-start.4 = ((f32[8,64,128]{2,1,0:T(8,128)}), f32[8,64,128]{2,1,0:T(8,128)S(1)}, u32[]{:S(2)}, u32[]{:S(2)}) async-start(f32[8,64,128]{2,1,0:T(8,128)} %broadcast_in_dim.136), calls=%async_computation.4 | async-start | bytes 524288 | tf_op jit(solution)/shard_map/all_to_all | solution.py:26
  158.3 23.4 %all-to-all-start.5 = ((f32[32,80,128]{2,1,0:T(8,128)}), f32[32,80,128]{2,1,0:T(8,128)S(1)}, u32[]{:S(2)}, u32[]{:S(2)}) async-start(f32[32,80,128]{2,1,0:T(8,128)} %broadcast_in_dim.140), calls=%async_computation.5 | async-start | bytes 2621440 | tf_op jit(solution)/shard_map/all_to_all | solution.py:170
